TPU v7x, 1024 devices: a whole 4x8x16 slice. The times are simulated.
1024 devices in a mesh: stretch: 16 (over y_hi, x, core), ctx: 64 (over y_lo, z).
Axes of the slice: x: 4, y: 8 (y_hi: 2, y_lo: 4; y = y_hi * 4 + y_lo), z: 16, core: 2. Of those that a mesh axis runs over, the one named last changes fastest.
Arguments:
- hidden_in: bfloat16 [131072, 5120], P(('stretch', 'ctx')), may hold values from -6 to 6
- query_weight: bfloat16 [5120, 384], P('ctx', 'stretch'), may hold values from -0.078125 to 0.078125
- stored_keys: bfloat16 [131072, 128], P(('stretch', 'ctx')), may hold values from -6 to 6
- stored_values: bfloat16 [131072, 128], P(('stretch', 'ctx')), may hold values from -6 to 6
- kv_scale: bfloat16 [131072, 2], P(('stretch', 'ctx')), may hold values from 0.25 to 64
- doc_start: int32 [131072], P(('stretch', 'ctx')), may hold values from 0 to 8191, as said below
Outputs:
- attended: bfloat16 [131072, 384], P(('stretch', 'ctx'))
Inputs may be any that keep to these rules, and one draw needn't show every extreme that they name: doc_start of a token is at most the token's own index inside its window, equals it at the first token of a document, is 0 at a window's first token and stays constant through a document; the last token of the first window is a document of its own.
All inputs are finite; a program needn't handle non-finite values.
Results may differ from a plain program's by a relative error of at most 0.0085.
The roundings to bfloat16 on the way count: a program that leaves them out, or rounds other values in their place, can miss the bound.
Values may be sent and summed in bfloat16 or wider, within the bound.
No kernel may reach another device: no remote copies, remote signals or barrier semaphores. Data moves between devices by JAX's collectives and lax.ppermute only.
A program may use at most 32 MiB of HBM per device.

v0:
```python
import math

import jax
import jax.numpy as jnp
from jax import lax
from jax.sharding import PartitionSpec as P

HEAD_DIM = 128
QUERY_HEADS = 3


def make_attend(q_set, pos_set, doc_set):

    def attend(carry, pieces, start):
        keys_raw, values_raw, scales = pieces
        count = keys_raw.shape[0]
        block = math.gcd(count, 512)
        keys = (keys_raw.astype(jnp.float32) * scales[:, 0:1].astype(jnp.float32)).astype(
            jnp.bfloat16
        )
        values = (values_raw.astype(jnp.float32) * scales[:, 1:2].astype(jnp.float32)).astype(
            jnp.bfloat16
        )

        def step(state, number):
            key_block = lax.dynamic_slice_in_dim(keys, number * block, block, 0)
            value_block = lax.dynamic_slice_in_dim(values, number * block, block, 0)
            columns = number * block + jnp.arange(block, dtype=jnp.int32)
            allowed = (columns[None, :] >= doc_set[:, None]) & (
                columns[None, :] <= pos_set[:, None]
            )
            scores = jnp.einsum("hqd,kd->hqk", q_set, key_block, preferred_element_type=jnp.float32)
            scores = jnp.where(allowed[None], scores, -1e30)
            top_old, total_old, accum = state
            top_new = jnp.maximum(top_old, jnp.max(scores, axis=2))
            weights = jnp.where(allowed[None], jnp.exp(scores - top_new[..., None]), 0.0)
            fade = jnp.exp(top_old - top_new)
            total_new = total_old * fade + jnp.sum(weights, axis=2)
            accum = accum * fade[..., None] + jnp.einsum(
                "hqk,kd->hqd",
                weights.astype(jnp.bfloat16),
                value_block,
                preferred_element_type=jnp.float32,
            )
            return ((top_new, total_new, accum), None)

        state, _ = lax.scan(step, carry, jnp.arange(count // block))
        return state

    return attend


def shards(hidden_in, query_weight, stored_keys, stored_values, kv_scale, doc_start):
    rows = hidden_in.shape[0]
    panel = lax.all_gather(query_weight, "stretch", axis=1, tiled=True)
    projected = jnp.dot(
        hidden_in,
        lax.all_gather(panel, "ctx", axis=0, tiled=True),
        preferred_element_type=jnp.float32,
    )
    queries = (projected * HEAD_DIM ** (-0.5)).astype(jnp.bfloat16)
    queries = jnp.transpose(queries.reshape(rows, QUERY_HEADS, HEAD_DIM), (1, 0, 2))
    position = lax.axis_index("ctx") * rows + jnp.arange(rows, dtype=jnp.int32)
    attend = make_attend(queries, position, doc_start)
    initial = (
        jnp.full((QUERY_HEADS, rows), -1e30, jnp.float32),
        jnp.zeros((QUERY_HEADS, rows), jnp.float32),
        jnp.zeros((QUERY_HEADS, rows, HEAD_DIM), jnp.float32),
    )
    top_final, total_final, accum_final = attend(
        initial,
        (
            lax.all_gather(stored_keys, "ctx", axis=0, tiled=True),
            lax.all_gather(stored_values, "ctx", axis=0, tiled=True),
            lax.all_gather(kv_scale, "ctx", axis=0, tiled=True),
        ),
        jnp.int32(0),
    )
    mixed = (accum_final / total_final[..., None]).astype(jnp.bfloat16)
    flat = jnp.transpose(mixed, (1, 0, 2)).reshape(rows, QUERY_HEADS * HEAD_DIM)
    return flat


def solution(mesh):
    return jax.shard_map(
        shards,
        mesh=mesh,
        in_specs=(
            P(("stretch", "ctx"), None),
            P("ctx", "stretch"),
            P(("stretch", "ctx"), None),
            P(("stretch", "ctx"), None),
            P(("stretch", "ctx"), None),
            P(("stretch", "ctx")),
        ),
        out_specs=P(("stretch", "ctx"), None),
        check_vma=False,
    )
```

profile of v0, /device:TPU:2, one launch (start us, length us, event | category | flops | bytes accessed | tf_op | source)
XLA Modules:
  0.0 985.6 jit_solution(15903388167688186344)
XLA Ops:
  6.5 0.7 all-gather.4.cloned.1.call-update
  7.3 0.7 all-gather.8.cloned.1.call-update
  8.1 37.4 %all_gather.17 = bf16[80,384]{0,1:T(8,128)(2,1)S(1)} all-gather(bf16[80,24]{0,1:T(8,128)(2,1)} %param.9), channel_id=1, replica_groups=mesh['stretch'=16,'ctx'=64] {'stretch'}, dimensions={1}, use_global_device_ids=true | all-gather | bytes 65280 | tf_op jit(solution)/shard_map/all_gather | solution.py:55
  45.4 0.7 copy.22
  46.2 151.9 %all_gather.16 = bf16[8192,2]{0,1:T(2,128)(2,1)S(1)} all-gather(bf16[128,2]{0,1:T(2,128)(2,1)} %param.12), channel_id=1, replica_groups=mesh['stretch'=16,'ctx'=64] {'ctx'}, dimensions={0}, use_global_device_ids=true | all-gather | bytes 33280 | tf_op jit(solution)/shard_map/all_gather | solution.py:75
  198.1 120.9 %all-gather.4.cloned.1.call-done = bf16[8192,128]{1,0:T(8,128)(2,1)} async-done(((bf16[128,128]{1,0:T(8,128)(2,1)}), bf16[8192,128]{1,0:T(8,128)(2,1)}) %all-gather.4.cloned.1.call-update) | async-done | bytes 2097168 | tf_op jit(solution)/shard_map/all_gather | solution.py:73
  319.0 3.4 multiply_convert_fusion.1
  322.5 290.3 %all-gather.8.cloned.1.call-done = bf16[8192,128]{1,0:T(8,128)(2,1)} async-done(((bf16[128,128]{1,0:T(8,128)(2,1)}), bf16[8192,128]{1,0:T(8,128)(2,1)}) %all-gather.8.cloned.1.call-update) | async-done | bytes 2097168 | tf_op jit(solution)/shard_map/all_gather | solution.py:74
  612.8 3.4 multiply_convert_fusion
  616.2 292.7 %all-gather.6.cloned.1.call-done = bf16[5120,384]{1,0:T(8,128)(2,1)} async-done(((bf16[80,384]{1,0:T(8,128)(2,1)}), bf16[5120,384]{1,0:T(8,128)(2,1)}) %all-gather.6.cloned.1.call-update) | async-done | bytes 3932176 | tf_op jit(solution)/shard_map/all_gather | solution.py:58
  908.9 3.0 fusion.17
  912.2 66.0 %while.15 = (s32[]{:T(128)}, f32[3,128]{1,0:T(4,128)S(1)}, f32[3,128]{1,0:T(4,128)S(1)}, f32[3,128,128]{2,1,0:T(8,128)S(1)}, s32[16]{0:T(128)S(1)}, /*index=5*/s...) while((s32[]{:T(128)}, f32[3,128]{1,0:T(4,128)S(1)}, ...), condition=%wide.region_3.4_spmd.clone, body=%wide.region_0.3_spmd.clone.sunk | while | flops 102582784 | bytes 3405539 | solution.py:47
  912.2 0.6 dynamic_slice.28
  913.6 1.2 fusion.31
  914.8 0.2 fusion.32
  915.0 1.3 convolution_add_fusion.2
  916.3 0.6 dynamic_slice.28
  917.7 1.2 fusion.31
  918.9 0.2 fusion.32
  919.1 1.3 convolution_add_fusion.2
  920.4 0.6 dynamic_slice.28
  921.8 1.2 fusion.31
  923.2 1.3 convolution_add_fusion.2
  924.6 0.6 dynamic_slice.28
  926.0 1.2 fusion.31
  927.4 1.3 convolution_add_fusion.2
  928.7 0.6 dynamic_slice.28
  930.1 1.2 fusion.31
  931.5 1.3 convolution_add_fusion.2
  932.8 0.6 dynamic_slice.28
  934.2 1.2 fusion.31
  935.6 1.3 convolution_add_fusion.2
  936.9 0.6 dynamic_slice.28
  938.4 1.2 fusion.31
  939.6 0.2 fusion.32
  939.8 1.3 convolution_add_fusion.2
  941.1 0.6 dynamic_slice.28
  942.5 1.2 fusion.31
  943.9 1.3 convolution_add_fusion.2
  945.2 0.6 dynamic_slice.28
  946.6 1.2 fusion.31
  948.0 1.3 convolution_add_fusion.2
  949.3 0.6 dynamic_slice.28
  950.7 1.2 fusion.31
  952.1 1.3 convolution_add_fusion.2
  953.4 0.6 dynamic_slice.28
  954.9 1.2 fusion.31
  956.3 1.3 convolution_add_fusion.2
  957.6 0.6 dynamic_slice.28
  959.0 1.2 fusion.31
  960.4 1.3 convolution_add_fusion.2
  961.7 0.6 dynamic_slice.28
  963.1 1.2 fusion.31
  964.5 1.3 convolution_add_fusion.2
  965.8 0.6 dynamic_slice.28
  967.2 1.2 fusion.31
  968.6 1.3 convolution_add_fusion.2
  970.0 0.6 dynamic_slice.28
  971.4 1.2 fusion.31
  972.8 1.3 convolution_add_fusion.2
  974.1 0.6 dynamic_slice.28
  975.5 1.2 fusion.31
  976.9 1.3 convolution_add_fusion.2
  978.4 0.8 copy.26
  (126 shorter events, 5.5 us)
Async XLA Ops:
  6.5 902.4 %copy-start = (bf16[128,5120]{1,0:T(8,128)(2,1)S(1)}, bf16[128,5120]{1,0:T(8,128)(2,1)}, u32[]{:S(2)}) copy-start(bf16[128,5120]{1,0:T(8,128)(2,1)} %param.8) | copy-start | bytes 3932164
  6.5 312.5 %all-gather.4.cloned.1.call-start = ((), (), s32[]{:S(2)}) async-start(), calls=%async_computation | async-start | bytes 2129920 | tf_op jit(solution)/shard_map/all_gather | solution.py:73
  7.3 605.6 %all-gather.8.cloned.1.call-start = ((), (), s32[]{:S(2)}) async-start(), calls=%async_computation.2 | async-start | bytes 2129920 | tf_op jit(solution)/shard_map/all_gather | solution.py:74
  8.0 900.9 %all-gather.6.cloned.1.call-start = ((), (), s32[]{:S(2)}) async-start(), calls=%async_computation.1 | async-start | bytes 3993600 | tf_op jit(solution)/shard_map/all_gather | solution.py:58
  616.2 295.9 %copy-start.1 = (s32[128]{0:T(128)S(1)}, s32[128]{0:T(128)}, u32[]{:S(2)}) copy-start(s32[128]{0:T(128)} %param.13) | copy-start | bytes 1540
Sparse Core Ops, SparseCore 0:
  10.0 308.9 all-gather.3
  321.7 291.0 all-gather.7
  615.5 293.3 all-gather.5
where the time goes:
time: 987 us; the launch traced here: 986 us
  waiting for transfers between devices  705 us (71%)
  blocking collectives  189 us (19%)
  matrix products  42.6 us (4%)
  between operations  13.2 us (1%)
  other arithmetic  12.3 us (1%)
  loops' own time  11.6 us (1%)
  local copies, waits for them, and re-layouts  11.3 us (1%)
    all_gather x1, waiting for transfers between devices, shards(): lax.all_gather(panel, 'ctx', axis=0, tiled=True)  293 us
    all_gather x1, waiting for transfers between devices, shards(): lax.all_gather(stored_values, 'ctx', axis=0, tiled=True)  290 us
    all_gather x1, blocking collectives, shards(): lax.all_gather(kv_scale, 'ctx', axis=0, tiled=True)  152 us
    all_gather x1, waiting for transfers between devices, shards(): lax.all_gather(stored_keys, 'ctx', axis=0, tiled=True)  121 us
    all_gather x1, blocking collectives, shards(): panel = lax.all_gather(query_weight, 'stretch', axis=1, tiled=True)  37.4 us
    dot_general x16, matrix products, step(): jnp.einsum('hqk,kd->hqd', weights.astype(jnp.bfloat16), value_block, pref...  20.6 us
  transfers between devices with their start and end apart: 3, of which 3 were waited for; matrix products, arithmetic and copies ran while one was open for 1% of the time, Pallas kernels for 0%

commit v1 on v0

--- a/solution.py
+++ b/solution.py
@@ -7,25 +7,21 @@
 
 HEAD_DIM = 128
 QUERY_HEADS = 3
+Z_RING = 16
+FAR = 1 << 24
 
 
 def make_attend(q_set, pos_set, doc_set):
 
-    def attend(carry, pieces, start):
-        keys_raw, values_raw, scales = pieces
-        count = keys_raw.shape[0]
+    def attend(carry, pieces):
+        keys, values, key_pos = pieces
+        count = keys.shape[0]
         block = math.gcd(count, 512)
-        keys = (keys_raw.astype(jnp.float32) * scales[:, 0:1].astype(jnp.float32)).astype(
-            jnp.bfloat16
-        )
-        values = (values_raw.astype(jnp.float32) * scales[:, 1:2].astype(jnp.float32)).astype(
-            jnp.bfloat16
-        )
 
         def step(state, number):
             key_block = lax.dynamic_slice_in_dim(keys, number * block, block, 0)
             value_block = lax.dynamic_slice_in_dim(values, number * block, block, 0)
-            columns = number * block + jnp.arange(block, dtype=jnp.int32)
+            columns = lax.dynamic_slice_in_dim(key_pos, number * block, block, 0)
             allowed = (columns[None, :] >= doc_set[:, None]) & (
                 columns[None, :] <= pos_set[:, None]
             )
@@ -50,14 +46,60 @@
     return attend
 
 
-def shards(hidden_in, query_weight, stored_keys, stored_values, kv_scale, doc_start):
+def gather_window(kv, n_ctx):
+    z_ring = Z_RING if n_ctx % Z_RING == 0 else n_ctx
+    rows = n_ctx // z_ring
+    me = lax.axis_index("ctx")
+    row, col = me // z_ring, me % z_ring
+    stack = [kv]
+    for k in range(1, rows):
+        perm = [(c, c + k * z_ring) for c in range(n_ctx - k * z_ring)]
+        stack.append(lax.ppermute(kv, "ctx", perm))
+    stack = jnp.stack(stack)
+    sources = [(0, 0)]
+    got = [stack]
+    fwd, bwd = stack, stack
+    half = z_ring // 2
+    for t in range(1, half + 1):
+        fwd = lax.ppermute(
+            fwd, "ctx", [(c, (c // z_ring) * z_ring + (c % z_ring + 1) % z_ring) for c in range(n_ctx)]
+        )
+        got.append(fwd)
+        sources.append((t, -1))
+        if t < z_ring - half:
+            bwd = lax.ppermute(
+                bwd, "ctx", [(c, (c // z_ring) * z_ring + (c % z_ring - 1) % z_ring) for c in range(n_ctx)]
+            )
+            got.append(bwd)
+            sources.append((t, 1))
+    blocks = jnp.stack(got)
+    shift = jnp.array([t * d for t, d in sources], jnp.int32)
+    src_col = (col + shift) % z_ring
+    src_row = row - jnp.arange(rows, dtype=jnp.int32)
+    src = src_row[None, :] * z_ring + src_col[:, None]
+    valid = src_row[None, :] >= 0
+    tokens = kv.shape[0]
+    key_pos = src[:, :, None] * tokens + jnp.arange(tokens, dtype=jnp.int32)
+    key_pos = jnp.where(valid[:, :, None], key_pos, FAR)
+    return blocks.reshape(-1, kv.shape[1]), key_pos.reshape(-1)
+
+
+def gather_weight(query_weight, n_ctx):
+    spread = jnp.broadcast_to(query_weight[None], (n_ctx,) + query_weight.shape)
+    rows = lax.all_to_all(spread, "ctx", 0, 0, tiled=False)
+    rows = rows.reshape(-1, query_weight.shape[1])
+    return lax.all_gather(rows, "stretch", axis=1, tiled=True)
+
+
+def shards(hidden_in, query_weight, stored_keys, stored_values, kv_scale, doc_start, n_ctx):
     rows = hidden_in.shape[0]
-    panel = lax.all_gather(query_weight, "stretch", axis=1, tiled=True)
-    projected = jnp.dot(
-        hidden_in,
-        lax.all_gather(panel, "ctx", axis=0, tiled=True),
-        preferred_element_type=jnp.float32,
+    keys = (stored_keys.astype(jnp.float32) * kv_scale[:, 0:1].astype(jnp.float32)).astype(jnp.bfloat16)
+    values = (stored_values.astype(jnp.float32) * kv_scale[:, 1:2].astype(jnp.float32)).astype(
+        jnp.bfloat16
     )
+    kv_all, key_pos = gather_window(jnp.concatenate([keys, values], axis=1), n_ctx)
+    weight = gather_weight(query_weight, n_ctx)
+    projected = jnp.dot(hidden_in, weight, preferred_element_type=jnp.float32)
     queries = (projected * HEAD_DIM ** (-0.5)).astype(jnp.bfloat16)
     queries = jnp.transpose(queries.reshape(rows, QUERY_HEADS, HEAD_DIM), (1, 0, 2))
     position = lax.axis_index("ctx") * rows + jnp.arange(rows, dtype=jnp.int32)
@@ -67,14 +109,9 @@
         jnp.zeros((QUERY_HEADS, rows), jnp.float32),
         jnp.zeros((QUERY_HEADS, rows, HEAD_DIM), jnp.float32),
     )
+    width = stored_keys.shape[1]
     top_final, total_final, accum_final = attend(
-        initial,
-        (
-            lax.all_gather(stored_keys, "ctx", axis=0, tiled=True),
-            lax.all_gather(stored_values, "ctx", axis=0, tiled=True),
-            lax.all_gather(kv_scale, "ctx", axis=0, tiled=True),
-        ),
-        jnp.int32(0),
+        initial, (kv_all[:, :width], kv_all[:, width:], key_pos)
     )
     mixed = (accum_final / total_final[..., None]).astype(jnp.bfloat16)
     flat = jnp.transpose(mixed, (1, 0, 2)).reshape(rows, QUERY_HEADS * HEAD_DIM)
@@ -82,8 +119,13 @@
 
 
 def solution(mesh):
+    n_ctx = mesh.shape["ctx"]
+
+    def body(*args):
+        return shards(*args, n_ctx=n_ctx)
+
     return jax.shard_map(
-        shards,
+        body,
         mesh=mesh,
         in_specs=(
             P(("stretch", "ctx"), None),

time: 987 us -> 238 us (0.24)
  the two profiles are of different devices: /device:TPU:2 before, /device:TPU:24 now
where the time goes in v1:
time: 238 us; the launch traced here: 237 us
  starting transfers between devices  56.6 us (24%)
  blocking collectives  48.9 us (21%)
  matrix products  43.1 us (18%)
  waiting for transfers between devices  38.5 us (16%)
  local copies, waits for them, and re-layouts  17.1 us (7%)
  between operations  13.9 us (6%)
  loops' own time  11.1 us (5%)
  other arithmetic  7.8 us (3%)
    all_to_all x1, blocking collectives, gather_weight(): rows = lax.all_to_all(spread, 'ctx', 0, 0, tiled=False)  48.9 us
    ppermute x7, starting transfers between devices, gather_window(): lax.ppermute(bwd, 'ctx', [(c, c // z_ring * z_ring + (c % z_ring - 1) % z...  36.6 us
    ppermute x8, waiting for transfers between devices, gather_window(): lax.ppermute(fwd, 'ctx', [(c, c // z_ring * z_ring + (c % z_ring + 1) % z...  31.2 us
    dot_general x16, matrix products, step(): jnp.einsum('hqk,kd->hqd', weights.astype(jnp.bfloat16), value_block, pref...  20.6 us
    dot_general x16, matrix products, step(): jnp.einsum('hqd,kd->hqk', q_set, key_block, preferred_element_type=jnp.fl...  19 us
    ppermute x8, starting transfers between devices, gather_window(): lax.ppermute(fwd, 'ctx', [(c, c // z_ring * z_ring + (c % z_ring + 1) % z...  16.1 us
    another operation x1, loops' own time, attend(): state, _ = lax.scan(step, carry, jnp.arange(count // block))  11.1 us
    dynamic_slice x16, local copies, waits for them, and re-layouts, attend(): state, _ = lax.scan(step, carry, jnp.arange(count // block))  9.92 us
  transfers between devices with their start and end apart: 19, of which 12 were waited for; matrix products, arithmetic and copies ran while one was open for 2% of the time, Pallas kernels for 0%

profile of v1, /device:TPU:24, one launch (start us, length us, event | category | flops | bytes accessed | tf_op | source)
XLA Modules:
  0.0 236.9 jit_solution(12711299939195790274)
XLA Ops:
  7.4 48.9 %all_to_all.5 = bf16[64,80,24]{1,2,0:T(8,128)(2,1)S(1)} all-to-all(bf16[64,80,24]{1,2,0:T(8,128)(2,1)S(1)} %broadcast_in_dim.65), channel_id=1, replica_groups=mesh['stretch'=16,'ctx'=64] {'ctx'}, dimensions={0} | all-to-all | bytes 491520 | tf_op jit(solution)/shard_map/all_to_all | solution.py:89
  56.3 1.3 reshape.122
  59.3 1.3 collective-permute-start
  60.6 1.3 collective-permute-start.1
  61.9 1.3 collective-permute-start.2
  64.0 1.4 collective-permute-done
  65.5 2.8 %collective-permute-done.1 = bf16[128,256]{1,0:T(8,128)(2,1)S(1)} collective-permute-done((bf16[128,256]{1,0:T(8,128)(2,1)S(1)}, bf16[128,256]{1,0:T(8,128)(2,1)S(1)}, u32[]{:S(2)}, u32[]{:S(2)}) %collective-permute-start.1) | collective-permute-done | bytes 65568 | tf_op jit(solution)/shard_map/ppermute | solution.py:57
  68.3 2.8 %collective-permute-done.2 = bf16[128,256]{1,0:T(8,128)(2,1)S(1)} collective-permute-done((bf16[128,256]{1,0:T(8,128)(2,1)S(1)}, bf16[128,256]{1,0:T(8,128)(2,1)S(1)}, u32[]{:S(2)}, u32[]{:S(2)}) %collective-permute-start.2) | collective-permute-done | bytes 65568 | tf_op jit(solution)/shard_map/ppermute | solution.py:57
  71.1 2.8 %collective-permute-start.3 = (bf16[4,128,256]{2,1,0:T(8,128)(2,1)S(1)}, bf16[4,128,256]{2,1,0:T(8,128)(2,1)S(1)}, u32[]{:S(2)}, u32[]{:S(2)}) collective-permute-start(bf16[4,128,256]{2,1,0:T(8,128)(2,1)S(1)} %pad_maximum_fusion), channel_id=1, source_target_pairs={{0,1},{1,2},{2,3},{3,4},{4,5},{5,6},{6,7},{7,8},{8,9},{9,10},{10,1... | collective-permute-start | bytes 786440 | tf_op jit(solution)/shard_map/ppermute | solution.py:64
  74.0 4.3 %collective-permute-start.4 = (bf16[4,128,256]{2,1,0:T(8,128)(2,1)S(1)}, bf16[4,128,256]{2,1,0:T(8,128)(2,1)S(1)}, u32[]{:S(2)}, u32[]{:S(2)}) collective-permute-start(bf16[4,128,256]{2,1,0:T(8,128)(2,1)S(1)} %pad_maximum_fusion), channel_id=1, source_target_pairs={{0,15},{1,0},{2,1},{3,2},{4,3},{5,4},{6,5},{7,6},{8,7},{9,8},{10,9... | collective-permute-start | bytes 786440 | tf_op jit(solution)/shard_map/ppermute | solution.py:70
  78.3 2.3 collective-permute-done.3
  80.6 1.9 collective-permute-start.5
  82.5 5.2 %collective-permute-start.6 = (bf16[4,128,256]{2,1,0:T(8,128)(2,1)S(1)}, bf16[4,128,256]{2,1,0:T(8,128)(2,1)S(1)}, u32[]{:S(2)}, u32[]{:S(2)}) collective-permute-start(bf16[4,128,256]{2,1,0:T(8,128)(2,1)S(1)} %collective-permute-done.4), channel_id=1, source_target_pairs={{0,15},{1,0},{2,1},{3,2},{4,3},{5,4},{6,5},{7,6},{8,7},{9,8},{10,9... | collective-permute-start | bytes 786440 | tf_op jit(solution)/shard_map/ppermute | solution.py:70
  87.7 2.3 collective-permute-done.5
  90.0 1.9 collective-permute-start.7
  92.0 5.3 %collective-permute-start.8 = (bf16[4,128,256]{2,1,0:T(8,128)(2,1)S(1)}, bf16[4,128,256]{2,1,0:T(8,128)(2,1)S(1)}, u32[]{:S(2)}, u32[]{:S(2)}) collective-permute-start(bf16[4,128,256]{2,1,0:T(8,128)(2,1)S(1)} %collective-permute-done.6), channel_id=1, source_target_pairs={{0,15},{1,0},{2,1},{3,2},{4,3},{5,4},{6,5},{7,6},{8,7},{9,8},{10,9... | collective-permute-start | bytes 786440 | tf_op jit(solution)/shard_map/ppermute | solution.py:70
  97.3 3.2 %collective-permute-done.7 = bf16[4,128,256]{2,1,0:T(8,128)(2,1)S(1)} collective-permute-done((bf16[4,128,256]{2,1,0:T(8,128)(2,1)S(1)}, bf16[4,128,256]{2,1,0:T(8,128)(2,1)S(1)}, u32[]{:S(2)}, u32[]{:S(2)}) %collective-permute-start.7) | collective-permute-done | bytes 262176 | tf_op jit(solution)/shard_map/ppermute | solution.py:64
  100.4 1.9 collective-permute-start.9
  102.4 5.5 %collective-permute-start.10 = (bf16[4,128,256]{2,1,0:T(8,128)(2,1)S(1)}, bf16[4,128,256]{2,1,0:T(8,128)(2,1)S(1)}, u32[]{:S(2)}, u32[]{:S(2)}) collective-permute-start(bf16[4,128,256]{2,1,0:T(8,128)(2,1)S(1)} %collective-permute-done.8), channel_id=1, source_target_pairs={{0,15},{1,0},{2,1},{3,2},{4,3},{5,4},{6,5},{7,6},{8,7},{9,8},{10,9... | collective-permute-start | bytes 786440 | tf_op jit(solution)/shard_map/ppermute | solution.py:70
  108.0 4.0 %collective-permute-done.9 = bf16[4,128,256]{2,1,0:T(8,128)(2,1)S(1)} collective-permute-done((bf16[4,128,256]{2,1,0:T(8,128)(2,1)S(1)}, bf16[4,128,256]{2,1,0:T(8,128)(2,1)S(1)}, u32[]{:S(2)}, u32[]{:S(2)}) %collective-permute-start.9) | collective-permute-done | bytes 262176 | tf_op jit(solution)/shard_map/ppermute | solution.py:64
  112.0 1.9 collective-permute-start.11
  114.2 5.6 %collective-permute-start.12 = (bf16[4,128,256]{2,1,0:T(8,128)(2,1)S(1)}, bf16[4,128,256]{2,1,0:T(8,128)(2,1)S(1)}, u32[]{:S(2)}, u32[]{:S(2)}) collective-permute-start(bf16[4,128,256]{2,1,0:T(8,128)(2,1)S(1)} %collective-permute-done.10), channel_id=1, source_target_pairs={{0,15},{1,0},{2,1},{3,2},{4,3},{5,4},{6,5},{7,6},{8,7},{9,8},{10,9... | collective-permute-start | bytes 786440 | tf_op jit(solution)/shard_map/ppermute | solution.py:70
  119.8 4.5 %collective-permute-done.11 = bf16[4,128,256]{2,1,0:T(8,128)(2,1)S(1)} collective-permute-done((bf16[4,128,256]{2,1,0:T(8,128)(2,1)S(1)}, bf16[4,128,256]{2,1,0:T(8,128)(2,1)S(1)}, u32[]{:S(2)}, u32[]{:S(2)}) %collective-permute-start.11) | collective-permute-done | bytes 262176 | tf_op jit(solution)/shard_map/ppermute | solution.py:64
  124.2 1.9 collective-permute-start.13
  126.2 5.5 %collective-permute-start.14 = (bf16[4,128,256]{2,1,0:T(8,128)(2,1)S(1)}, bf16[4,128,256]{2,1,0:T(8,128)(2,1)S(1)}, u32[]{:S(2)}, u32[]{:S(2)}) collective-permute-start(bf16[4,128,256]{2,1,0:T(8,128)(2,1)S(1)} %collective-permute-done.12), channel_id=1, source_target_pairs={{0,15},{1,0},{2,1},{3,2},{4,3},{5,4},{6,5},{7,6},{8,7},{9,8},{10,9... | collective-permute-start | bytes 786440 | tf_op jit(solution)/shard_map/ppermute | solution.py:70
  131.8 4.0 %collective-permute-done.13 = bf16[4,128,256]{2,1,0:T(8,128)(2,1)S(1)} collective-permute-done((bf16[4,128,256]{2,1,0:T(8,128)(2,1)S(1)}, bf16[4,128,256]{2,1,0:T(8,128)(2,1)S(1)}, u32[]{:S(2)}, u32[]{:S(2)}) %collective-permute-start.13) | collective-permute-done | bytes 262176 | tf_op jit(solution)/shard_map/ppermute | solution.py:64
  135.7 1.9 collective-permute-start.15
  137.7 5.3 %collective-permute-start.16 = (bf16[4,128,256]{2,1,0:T(8,128)(2,1)S(1)}, bf16[4,128,256]{2,1,0:T(8,128)(2,1)S(1)}, u32[]{:S(2)}, u32[]{:S(2)}) collective-permute-start(bf16[4,128,256]{2,1,0:T(8,128)(2,1)S(1)} %collective-permute-done.14), channel_id=1, source_target_pairs={{0,15},{1,0},{2,1},{3,2},{4,3},{5,4},{6,5},{7,6},{8,7},{9,8},{10,9... | collective-permute-start | bytes 786440 | tf_op jit(solution)/shard_map/ppermute | solution.py:70
  143.0 3.5 %collective-permute-done.15 = bf16[4,128,256]{2,1,0:T(8,128)(2,1)S(1)} collective-permute-done((bf16[4,128,256]{2,1,0:T(8,128)(2,1)S(1)}, bf16[4,128,256]{2,1,0:T(8,128)(2,1)S(1)}, u32[]{:S(2)}, u32[]{:S(2)}) %collective-permute-start.15) | collective-permute-done | bytes 262176 | tf_op jit(solution)/shard_map/ppermute | solution.py:64
  146.5 1.9 collective-permute-start.17
  148.5 7.5 %collective-permute-done.17 = bf16[4,128,256]{2,1,0:T(8,128)(2,1)S(1)} collective-permute-done((bf16[4,128,256]{2,1,0:T(8,128)(2,1)S(1)}, bf16[4,128,256]{2,1,0:T(8,128)(2,1)S(1)}, u32[]{:S(2)}, u32[]{:S(2)}) %collective-permute-start.17) | collective-permute-done | bytes 262176 | tf_op jit(solution)/shard_map/ppermute | solution.py:64
  156.0 2.3 fusion.23
  158.2 3.4 %fusion.17 = bf16[128,384]{1,0:T(8,128)(2,1)S(1)} fusion(bf16[128,5120]{1,0:T(8,128)(2,1)S(1)} %copy-done, bf16[5120,384]{0,1:T(8,128)(2,1)} %all-gather.2.cloned.1.call-done), kind=kOutput, calls=%fused_computation.25 | convolution fusion | flops 503414784 | bytes 5341184 | tf_op jit(solution)/shard_map/dot_general | solution.py:102
  161.9 67.2 %while.15 = (s32[]{:T(128)}, f32[3,128]{1,0:T(4,128)S(1)}, f32[3,128]{1,0:T(4,128)S(1)}, f32[3,128,128]{2,1,0:T(8,128)S(1)}, s32[16]{0:T(128)S(1)}, /*index=5*/s...) while((s32[]{:T(128)}, f32[3,128]{1,0:T(4,128)S(1)}, ...), condition=%wide.region_3.4_spmd.clone, body=%wide.region_0.3_spmd.clone.sunk | while | flops 102582272 | bytes 3407587 | solution.py:43
  164.8 1.3 convolution_add_fusion.2
  167.6 1.2 fusion.36
  169.0 1.3 convolution_add_fusion.2
  171.8 1.2 fusion.36
  173.2 1.3 convolution_add_fusion.2
  176.0 1.2 fusion.36
  177.4 1.3 convolution_add_fusion.2
  180.2 1.2 fusion.36
  181.6 1.3 convolution_add_fusion.2
  184.4 1.2 fusion.36
  185.8 1.3 convolution_add_fusion.2
  188.6 1.2 fusion.36
  190.0 1.3 convolution_add_fusion.2
  192.8 1.2 fusion.36
  194.2 1.3 convolution_add_fusion.2
  197.0 1.2 fusion.36
  198.4 1.3 convolution_add_fusion.2
  201.2 1.2 fusion.36
  202.6 1.3 convolution_add_fusion.2
  205.4 1.2 fusion.36
  206.8 1.3 convolution_add_fusion.2
  209.6 1.2 fusion.36
  211.0 1.3 convolution_add_fusion.2
  213.8 1.2 fusion.36
  215.2 1.3 convolution_add_fusion.2
  218.0 1.2 fusion.36
  219.4 1.3 convolution_add_fusion.2
  223.6 1.3 convolution_add_fusion.2
  226.4 1.2 fusion.36
  227.8 1.3 convolution_add_fusion.2
  (180 shorter events, 24.0 us)
Async XLA Ops:
  6.5 151.7 %copy-start = (bf16[128,5120]{1,0:T(8,128)(2,1)S(1)}, bf16[128,5120]{1,0:T(8,128)(2,1)}, u32[]{:S(2)}) copy-start(bf16[128,5120]{1,0:T(8,128)(2,1)} %param.9) | copy-start | bytes 3932164
  6.5 151.7 %all-gather.2.cloned.1.call-start = ((), (), s32[]{:S(2)}) async-start(), calls=%async_computation.1 | async-start | bytes 4177920 | tf_op jit(solution)/shard_map/all_gather | solution.py:91
  59.3 6.2 %collective-permute-start = (bf16[128,256]{1,0:T(8,128)(2,1)S(1)}, bf16[128,256]{1,0:T(8,128)(2,1)S(1)}, u32[]{:S(2)}, u32[]{:S(2)}) collective-permute-start(bf16[128,256]{1,0:T(8,128)(2,1)S(1)} %get-tuple-element.166), channel_id=1, source_target_pairs={{0,16},{1,17},{2,18},{3,19},{4,20},{5,21},{6,22},{7,23},{8,24},{9,... | collective-permute-start | bytes 196616 | tf_op jit(solution)/shard_map/ppermute | solution.py:57
  60.6 7.7 %collective-permute-start.1 = (bf16[128,256]{1,0:T(8,128)(2,1)S(1)}, bf16[128,256]{1,0:T(8,128)(2,1)S(1)}, u32[]{:S(2)}, u32[]{:S(2)}) collective-permute-start(bf16[128,256]{1,0:T(8,128)(2,1)S(1)} %get-tuple-element.166), channel_id=1, source_target_pairs={{0,32},{1,33},{2,34},{3,35},{4,36},{5,37},{6,38},{7,39},{8,40},{9,... | collective-permute-start | bytes 196616 | tf_op jit(solution)/shard_map/ppermute | solution.py:57
  61.9 9.1 %collective-permute-start.2 = (bf16[128,256]{1,0:T(8,128)(2,1)S(1)}, bf16[128,256]{1,0:T(8,128)(2,1)S(1)}, u32[]{:S(2)}, u32[]{:S(2)}) collective-permute-start(bf16[128,256]{1,0:T(8,128)(2,1)S(1)} %get-tuple-element.166), channel_id=1, source_target_pairs={{0,48},{1,49},{2,50},{3,51},{4,52},{5,53},{6,54},{7,55},{8,56},{9,... | collective-permute-start | bytes 196616 | tf_op jit(solution)/shard_map/ppermute | solution.py:57
  71.1 9.5 %collective-permute-start.3 = (bf16[4,128,256]{2,1,0:T(8,128)(2,1)S(1)}, bf16[4,128,256]{2,1,0:T(8,128)(2,1)S(1)}, u32[]{:S(2)}, u32[]{:S(2)}) collective-permute-start(bf16[4,128,256]{2,1,0:T(8,128)(2,1)S(1)} %pad_maximum_fusion), channel_id=1, source_target_pairs={{0,1},{1,2},{2,3},{3,4},{4,5},{5,6},{6,7},{7,8},{8,9},{9,10},{10,1... | collective-permute-start | bytes 786440 | tf_op jit(solution)/shard_map/ppermute | solution.py:64
  74.0 8.5 %collective-permute-start.4 = (bf16[4,128,256]{2,1,0:T(8,128)(2,1)S(1)}, bf16[4,128,256]{2,1,0:T(8,128)(2,1)S(1)}, u32[]{:S(2)}, u32[]{:S(2)}) collective-permute-start(bf16[4,128,256]{2,1,0:T(8,128)(2,1)S(1)} %pad_maximum_fusion), channel_id=1, source_target_pairs={{0,15},{1,0},{2,1},{3,2},{4,3},{5,4},{6,5},{7,6},{8,7},{9,8},{10,9... | collective-permute-start | bytes 786440 | tf_op jit(solution)/shard_map/ppermute | solution.py:70
  80.6 9.5 %collective-permute-start.5 = (bf16[4,128,256]{2,1,0:T(8,128)(2,1)S(1)}, bf16[4,128,256]{2,1,0:T(8,128)(2,1)S(1)}, u32[]{:S(2)}, u32[]{:S(2)}) collective-permute-start(bf16[4,128,256]{2,1,0:T(8,128)(2,1)S(1)} %collective-permute-done.3), channel_id=1, source_target_pairs={{0,1},{1,2},{2,3},{3,4},{4,5},{5,6},{6,7},{7,8},{8,9},{9,10},{10,1... | collective-permute-start | bytes 786440 | tf_op jit(solution)/shard_map/ppermute | solution.py:64
  82.5 9.5 %collective-permute-start.6 = (bf16[4,128,256]{2,1,0:T(8,128)(2,1)S(1)}, bf16[4,128,256]{2,1,0:T(8,128)(2,1)S(1)}, u32[]{:S(2)}, u32[]{:S(2)}) collective-permute-start(bf16[4,128,256]{2,1,0:T(8,128)(2,1)S(1)} %collective-permute-done.4), channel_id=1, source_target_pairs={{0,15},{1,0},{2,1},{3,2},{4,3},{5,4},{6,5},{7,6},{8,7},{9,8},{10,9... | collective-permute-start | bytes 786440 | tf_op jit(solution)/shard_map/ppermute | solution.py:70
  90.0 10.4 %collective-permute-start.7 = (bf16[4,128,256]{2,1,0:T(8,128)(2,1)S(1)}, bf16[4,128,256]{2,1,0:T(8,128)(2,1)S(1)}, u32[]{:S(2)}, u32[]{:S(2)}) collective-permute-start(bf16[4,128,256]{2,1,0:T(8,128)(2,1)S(1)} %collective-permute-done.5), channel_id=1, source_target_pairs={{0,1},{1,2},{2,3},{3,4},{4,5},{5,6},{6,7},{7,8},{8,9},{9,10},{10,1... | collective-permute-start | bytes 786440 | tf_op jit(solution)/shard_map/ppermute | solution.py:64
  92.0 10.4 %collective-permute-start.8 = (bf16[4,128,256]{2,1,0:T(8,128)(2,1)S(1)}, bf16[4,128,256]{2,1,0:T(8,128)(2,1)S(1)}, u32[]{:S(2)}, u32[]{:S(2)}) collective-permute-start(bf16[4,128,256]{2,1,0:T(8,128)(2,1)S(1)} %collective-permute-done.6), channel_id=1, source_target_pairs={{0,15},{1,0},{2,1},{3,2},{4,3},{5,4},{6,5},{7,6},{8,7},{9,8},{10,9... | collective-permute-start | bytes 786440 | tf_op jit(solution)/shard_map/ppermute | solution.py:70
  100.4 11.5 %collective-permute-start.9 = (bf16[4,128,256]{2,1,0:T(8,128)(2,1)S(1)}, bf16[4,128,256]{2,1,0:T(8,128)(2,1)S(1)}, u32[]{:S(2)}, u32[]{:S(2)}) collective-permute-start(bf16[4,128,256]{2,1,0:T(8,128)(2,1)S(1)} %collective-permute-done.7), channel_id=1, source_target_pairs={{0,1},{1,2},{2,3},{3,4},{4,5},{5,6},{6,7},{7,8},{8,9},{9,10},{10,1... | collective-permute-start | bytes 786440 | tf_op jit(solution)/shard_map/ppermute | solution.py:64
  102.4 11.8 %collective-permute-start.10 = (bf16[4,128,256]{2,1,0:T(8,128)(2,1)S(1)}, bf16[4,128,256]{2,1,0:T(8,128)(2,1)S(1)}, u32[]{:S(2)}, u32[]{:S(2)}) collective-permute-start(bf16[4,128,256]{2,1,0:T(8,128)(2,1)S(1)} %collective-permute-done.8), channel_id=1, source_target_pairs={{0,15},{1,0},{2,1},{3,2},{4,3},{5,4},{6,5},{7,6},{8,7},{9,8},{10,9... | collective-permute-start | bytes 786440 | tf_op jit(solution)/shard_map/ppermute | solution.py:70
  112.0 12.2 %collective-permute-start.11 = (bf16[4,128,256]{2,1,0:T(8,128)(2,1)S(1)}, bf16[4,128,256]{2,1,0:T(8,128)(2,1)S(1)}, u32[]{:S(2)}, u32[]{:S(2)}) collective-permute-start(bf16[4,128,256]{2,1,0:T(8,128)(2,1)S(1)} %collective-permute-done.9), channel_id=1, source_target_pairs={{0,1},{1,2},{2,3},{3,4},{4,5},{5,6},{6,7},{7,8},{8,9},{9,10},{10,1... | collective-permute-start | bytes 786440 | tf_op jit(solution)/shard_map/ppermute | solution.py:64
  114.2 12.0 %collective-permute-start.12 = (bf16[4,128,256]{2,1,0:T(8,128)(2,1)S(1)}, bf16[4,128,256]{2,1,0:T(8,128)(2,1)S(1)}, u32[]{:S(2)}, u32[]{:S(2)}) collective-permute-start(bf16[4,128,256]{2,1,0:T(8,128)(2,1)S(1)} %collective-permute-done.10), channel_id=1, source_target_pairs={{0,15},{1,0},{2,1},{3,2},{4,3},{5,4},{6,5},{7,6},{8,7},{9,8},{10,9... | collective-permute-start | bytes 786440 | tf_op jit(solution)/shard_map/ppermute | solution.py:70
  124.2 11.5 %collective-permute-start.13 = (bf16[4,128,256]{2,1,0:T(8,128)(2,1)S(1)}, bf16[4,128,256]{2,1,0:T(8,128)(2,1)S(1)}, u32[]{:S(2)}, u32[]{:S(2)}) collective-permute-start(bf16[4,128,256]{2,1,0:T(8,128)(2,1)S(1)} %collective-permute-done.11), channel_id=1, source_target_pairs={{0,1},{1,2},{2,3},{3,4},{4,5},{5,6},{6,7},{7,8},{8,9},{9,10},{10,1... | collective-permute-start | bytes 786440 | tf_op jit(solution)/shard_map/ppermute | solution.py:64
  126.2 11.5 %collective-permute-start.14 = (bf16[4,128,256]{2,1,0:T(8,128)(2,1)S(1)}, bf16[4,128,256]{2,1,0:T(8,128)(2,1)S(1)}, u32[]{:S(2)}, u32[]{:S(2)}) collective-permute-start(bf16[4,128,256]{2,1,0:T(8,128)(2,1)S(1)} %collective-permute-done.12), channel_id=1, source_target_pairs={{0,15},{1,0},{2,1},{3,2},{4,3},{5,4},{6,5},{7,6},{8,7},{9,8},{10,9... | collective-permute-start | bytes 786440 | tf_op jit(solution)/shard_map/ppermute | solution.py:70
  135.7 10.7 %collective-permute-start.15 = (bf16[4,128,256]{2,1,0:T(8,128)(2,1)S(1)}, bf16[4,128,256]{2,1,0:T(8,128)(2,1)S(1)}, u32[]{:S(2)}, u32[]{:S(2)}) collective-permute-start(bf16[4,128,256]{2,1,0:T(8,128)(2,1)S(1)} %collective-permute-done.13), channel_id=1, source_target_pairs={{0,1},{1,2},{2,3},{3,4},{4,5},{5,6},{6,7},{7,8},{8,9},{9,10},{10,1... | collective-permute-start | bytes 786440 | tf_op jit(solution)/shard_map/ppermute | solution.py:64
  137.7 10.7 %collective-permute-start.16 = (bf16[4,128,256]{2,1,0:T(8,128)(2,1)S(1)}, bf16[4,128,256]{2,1,0:T(8,128)(2,1)S(1)}, u32[]{:S(2)}, u32[]{:S(2)}) collective-permute-start(bf16[4,128,256]{2,1,0:T(8,128)(2,1)S(1)} %collective-permute-done.14), channel_id=1, source_target_pairs={{0,15},{1,0},{2,1},{3,2},{4,3},{5,4},{6,5},{7,6},{8,7},{9,8},{10,9... | collective-permute-start | bytes 786440 | tf_op jit(solution)/shard_map/ppermute | solution.py:70
  146.5 9.5 %collective-permute-start.17 = (bf16[4,128,256]{2,1,0:T(8,128)(2,1)S(1)}, bf16[4,128,256]{2,1,0:T(8,128)(2,1)S(1)}, u32[]{:S(2)}, u32[]{:S(2)}) collective-permute-start(bf16[4,128,256]{2,1,0:T(8,128)(2,1)S(1)} %collective-permute-done.15), channel_id=1, source_target_pairs={{0,1},{1,2},{2,3},{3,4},{4,5},{5,6},{6,7},{7,8},{8,9},{9,10},{10,1... | collective-permute-start | bytes 786440 | tf_op jit(solution)/shard_map/ppermute | solution.py:64
  158.2 3.7 %copy-start.1 = (s32[128]{0:T(128)S(1)}, s32[128]{0:T(128)}, u32[]{:S(2)}) copy-start(s32[128]{0:T(128)} %param.14) | copy-start | bytes 1540
Sparse Core Ops, SparseCore 0:
  57.8 78.5 all-gather.1

commit v2 on v1

--- a/solution.py
+++ b/solution.py
@@ -16,7 +16,7 @@
     def attend(carry, pieces):
         keys, values, key_pos = pieces
         count = keys.shape[0]
-        block = math.gcd(count, 512)
+        block = count
 
         def step(state, number):
             key_block = lax.dynamic_slice_in_dim(keys, number * block, block, 0)

time: 238 us -> 192 us (0.81)
  the two profiles are of different devices: /device:TPU:24 before, /device:TPU:26 now
where the time goes in v2:
time: 192 us; the launch traced here: 191 us
  starting transfers between devices  56.9 us (30%)
  blocking collectives  48.9 us (25%)
  waiting for transfers between devices  25.9 us (13%)
  matrix products  19.6 us (10%)
  local copies, waits for them, and re-layouts  13.9 us (7%)
  between operations  13.7 us (7%)
  other arithmetic  12.4 us (6%)
    all_to_all x1, blocking collectives, gather_weight(): rows = lax.all_to_all(spread, 'ctx', 0, 0, tiled=False)  48.9 us
    ppermute x7, starting transfers between devices, gather_window(): lax.ppermute(bwd, 'ctx', [(c, c // z_ring * z_ring + (c % z_ring - 1) % z...  36.7 us
    ppermute x8, waiting for transfers between devices, gather_window(): lax.ppermute(fwd, 'ctx', [(c, c // z_ring * z_ring + (c % z_ring + 1) % z...  18.6 us
    ppermute x8, starting transfers between devices, gather_window(): lax.ppermute(fwd, 'ctx', [(c, c // z_ring * z_ring + (c % z_ring + 1) % z...  16.3 us
    unnamed x16, local copies, waits for them, and re-layouts  10.1 us
    dot_general x1, matrix products, step(): jnp.einsum('hqd,kd->hqk', q_set, key_block, preferred_element_type=jnp.fl...  8.3 us
    dot_general x1, matrix products, step(): jnp.einsum('hqk,kd->hqd', weights.astype(jnp.bfloat16), value_block, pref...  7.89 us
    reduce_sum x1, other arithmetic, step(): total_new = total_old * fade + jnp.sum(weights, axis=2)  7.57 us
  transfers between devices with their start and end apart: 19, of which 13 were waited for; matrix products, arithmetic and copies ran while one was open for 8% of the time, Pallas kernels for 0%

profile of v2, /device:TPU:26, one launch (start us, length us, event | category | flops | bytes accessed | tf_op | source)
XLA Modules:
  0.0 191.3 jit_solution(6537102556733467602)
XLA Ops:
  6.5 0.8 broadcast_in_dim.74
  7.4 48.9 %all_to_all.5 = bf16[64,80,24]{1,2,0:T(8,128)(2,1)S(1)} all-to-all(bf16[64,80,24]{1,2,0:T(8,128)(2,1)S(1)} %broadcast_in_dim.74), channel_id=1, replica_groups=mesh['stretch'=16,'ctx'=64] {'ctx'}, dimensions={0} | all-to-all | bytes 491520 | tf_op jit(solution)/shard_map/all_to_all | solution.py:89
  56.2 0.1 copy.21
  56.3 1.3 reshape.152
  57.6 0.0 all-gather.2.cloned.1.call-update
  57.7 0.7 bitcast_convert_fusion.1
  58.4 0.9 multiply_convert_fusion
  59.3 1.3 collective-permute-start.1
  60.6 1.3 collective-permute-start
  61.9 1.3 collective-permute-start.2
  63.2 0.7 and_select_fusion
  63.9 0.1 add_multiply_fusion
  64.0 0.1 add_select_fusion
  64.1 3.0 %collective-permute-done.1 = bf16[128,256]{1,0:T(8,128)(2,1)S(1)} collective-permute-done((bf16[128,256]{1,0:T(8,128)(2,1)S(1)}, bf16[128,256]{1,0:T(8,128)(2,1)S(1)}, u32[]{:S(2)}, u32[]{:S(2)}) %collective-permute-start.1) | collective-permute-done | bytes 65568 | tf_op jit(solution)/shard_map/ppermute | solution.py:57
  67.1 0.9 collective-permute-done
  68.0 3.1 %collective-permute-done.2 = bf16[128,256]{1,0:T(8,128)(2,1)S(1)} collective-permute-done((bf16[128,256]{1,0:T(8,128)(2,1)S(1)}, bf16[128,256]{1,0:T(8,128)(2,1)S(1)}, u32[]{:S(2)}, u32[]{:S(2)}) %collective-permute-start.2) | collective-permute-done | bytes 65568 | tf_op jit(solution)/shard_map/ppermute | solution.py:57
  71.1 2.8 %collective-permute-start.3 = (bf16[4,128,256]{2,1,0:T(8,128)(2,1)S(1)}, bf16[4,128,256]{2,1,0:T(8,128)(2,1)S(1)}, u32[]{:S(2)}, u32[]{:S(2)}) collective-permute-start(bf16[4,128,256]{2,1,0:T(8,128)(2,1)S(1)} %pad_maximum_fusion), channel_id=1, source_target_pairs={{0,1},{1,2},{2,3},{3,4},{4,5},{5,6},{6,7},{7,8},{8,9},{9,10},{10,1... | collective-permute-start | bytes 786440 | tf_op jit(solution)/shard_map/ppermute | solution.py:64
  73.9 4.3 %collective-permute-start.4 = (bf16[4,128,256]{2,1,0:T(8,128)(2,1)S(1)}, bf16[4,128,256]{2,1,0:T(8,128)(2,1)S(1)}, u32[]{:S(2)}, u32[]{:S(2)}) collective-permute-start(bf16[4,128,256]{2,1,0:T(8,128)(2,1)S(1)} %pad_maximum_fusion), channel_id=1, source_target_pairs={{0,15},{1,0},{2,1},{3,2},{4,3},{5,4},{6,5},{7,6},{8,7},{9,8},{10,9... | collective-permute-start | bytes 786440 | tf_op jit(solution)/shard_map/ppermute | solution.py:70
  78.1 1.5 compare_and_fusion
  79.7 0.8 bitcast_dynamic-update-slice_fusion.15
  80.4 0.1 collective-permute-done.3
  80.5 1.9 collective-permute-start.5
  82.5 5.1 %collective-permute-start.6 = (bf16[4,128,256]{2,1,0:T(8,128)(2,1)S(1)}, bf16[4,128,256]{2,1,0:T(8,128)(2,1)S(1)}, u32[]{:S(2)}, u32[]{:S(2)}) collective-permute-start(bf16[4,128,256]{2,1,0:T(8,128)(2,1)S(1)} %collective-permute-done.4), channel_id=1, source_target_pairs={{0,15},{1,0},{2,1},{3,2},{4,3},{5,4},{6,5},{7,6},{8,7},{9,8},{10,9... | collective-permute-start | bytes 786440 | tf_op jit(solution)/shard_map/ppermute | solution.py:70
  87.6 0.7 bitcast_dynamic-update-slice_fusion.14
  88.4 0.7 bitcast_dynamic-update-slice_fusion.13
  89.1 0.9 collective-permute-done.5
  90.0 1.9 collective-permute-start.7
  91.9 5.1 %collective-permute-start.8 = (bf16[4,128,256]{2,1,0:T(8,128)(2,1)S(1)}, bf16[4,128,256]{2,1,0:T(8,128)(2,1)S(1)}, u32[]{:S(2)}, u32[]{:S(2)}) collective-permute-start(bf16[4,128,256]{2,1,0:T(8,128)(2,1)S(1)} %collective-permute-done.6), channel_id=1, source_target_pairs={{0,15},{1,0},{2,1},{3,2},{4,3},{5,4},{6,5},{7,6},{8,7},{9,8},{10,9... | collective-permute-start | bytes 786440 | tf_op jit(solution)/shard_map/ppermute | solution.py:70
  97.1 0.7 bitcast_dynamic-update-slice_fusion.12
  97.8 0.7 bitcast_dynamic-update-slice_fusion.11
  98.5 1.7 collective-permute-done.7
  100.2 1.9 collective-permute-start.9
  102.1 5.4 %collective-permute-start.10 = (bf16[4,128,256]{2,1,0:T(8,128)(2,1)S(1)}, bf16[4,128,256]{2,1,0:T(8,128)(2,1)S(1)}, u32[]{:S(2)}, u32[]{:S(2)}) collective-permute-start(bf16[4,128,256]{2,1,0:T(8,128)(2,1)S(1)} %collective-permute-done.8), channel_id=1, source_target_pairs={{0,15},{1,0},{2,1},{3,2},{4,3},{5,4},{6,5},{7,6},{8,7},{9,8},{10,9... | collective-permute-start | bytes 786440 | tf_op jit(solution)/shard_map/ppermute | solution.py:70
  107.5 0.7 bitcast_dynamic-update-slice_fusion.10
  108.2 0.7 bitcast_dynamic-update-slice_fusion.9
  108.9 2.5 %collective-permute-done.9 = bf16[4,128,256]{2,1,0:T(8,128)(2,1)S(1)} collective-permute-done((bf16[4,128,256]{2,1,0:T(8,128)(2,1)S(1)}, bf16[4,128,256]{2,1,0:T(8,128)(2,1)S(1)}, u32[]{:S(2)}, u32[]{:S(2)}) %collective-permute-start.9) | collective-permute-done | bytes 262176 | tf_op jit(solution)/shard_map/ppermute | solution.py:64
  111.5 1.9 collective-permute-start.11
  113.4 0.1 collective-permute-done.10
  113.5 5.6 %collective-permute-start.12 = (bf16[4,128,256]{2,1,0:T(8,128)(2,1)S(1)}, bf16[4,128,256]{2,1,0:T(8,128)(2,1)S(1)}, u32[]{:S(2)}, u32[]{:S(2)}) collective-permute-start(bf16[4,128,256]{2,1,0:T(8,128)(2,1)S(1)} %collective-permute-done.10), channel_id=1, source_target_pairs={{0,15},{1,0},{2,1},{3,2},{4,3},{5,4},{6,5},{7,6},{8,7},{9,8},{10,9... | collective-permute-start | bytes 786440 | tf_op jit(solution)/shard_map/ppermute | solution.py:70
  119.1 0.7 bitcast_dynamic-update-slice_fusion.8
  119.9 0.7 bitcast_dynamic-update-slice_fusion.7
  120.6 3.0 %collective-permute-done.11 = bf16[4,128,256]{2,1,0:T(8,128)(2,1)S(1)} collective-permute-done((bf16[4,128,256]{2,1,0:T(8,128)(2,1)S(1)}, bf16[4,128,256]{2,1,0:T(8,128)(2,1)S(1)}, u32[]{:S(2)}, u32[]{:S(2)}) %collective-permute-start.11) | collective-permute-done | bytes 262176 | tf_op jit(solution)/shard_map/ppermute | solution.py:64
  123.5 1.9 collective-permute-start.13
  125.5 0.3 collective-permute-done.12
  125.7 5.6 %collective-permute-start.14 = (bf16[4,128,256]{2,1,0:T(8,128)(2,1)S(1)}, bf16[4,128,256]{2,1,0:T(8,128)(2,1)S(1)}, u32[]{:S(2)}, u32[]{:S(2)}) collective-permute-start(bf16[4,128,256]{2,1,0:T(8,128)(2,1)S(1)} %collective-permute-done.12), channel_id=1, source_target_pairs={{0,15},{1,0},{2,1},{3,2},{4,3},{5,4},{6,5},{7,6},{8,7},{9,8},{10,9... | collective-permute-start | bytes 786440 | tf_op jit(solution)/shard_map/ppermute | solution.py:70
  131.3 0.7 bitcast_dynamic-update-slice_fusion.6
  132.1 0.7 bitcast_dynamic-update-slice_fusion.5
  132.8 2.5 %collective-permute-done.13 = bf16[4,128,256]{2,1,0:T(8,128)(2,1)S(1)} collective-permute-done((bf16[4,128,256]{2,1,0:T(8,128)(2,1)S(1)}, bf16[4,128,256]{2,1,0:T(8,128)(2,1)S(1)}, u32[]{:S(2)}, u32[]{:S(2)}) %collective-permute-start.13) | collective-permute-done | bytes 262176 | tf_op jit(solution)/shard_map/ppermute | solution.py:64
  135.3 1.9 collective-permute-start.15
  137.2 5.6 %collective-permute-start.16 = (bf16[4,128,256]{2,1,0:T(8,128)(2,1)S(1)}, bf16[4,128,256]{2,1,0:T(8,128)(2,1)S(1)}, u32[]{:S(2)}, u32[]{:S(2)}) collective-permute-start(bf16[4,128,256]{2,1,0:T(8,128)(2,1)S(1)} %collective-permute-done.14), channel_id=1, source_target_pairs={{0,15},{1,0},{2,1},{3,2},{4,3},{5,4},{6,5},{7,6},{8,7},{9,8},{10,9... | collective-permute-start | bytes 786440 | tf_op jit(solution)/shard_map/ppermute | solution.py:70
  142.8 0.7 bitcast_dynamic-update-slice_fusion.4
  143.5 0.7 bitcast_dynamic-update-slice_fusion.3
  144.2 2.0 %collective-permute-done.15 = bf16[4,128,256]{2,1,0:T(8,128)(2,1)S(1)} collective-permute-done((bf16[4,128,256]{2,1,0:T(8,128)(2,1)S(1)}, bf16[4,128,256]{2,1,0:T(8,128)(2,1)S(1)}, u32[]{:S(2)}, u32[]{:S(2)}) %collective-permute-start.15) | collective-permute-done | bytes 262176 | tf_op jit(solution)/shard_map/ppermute | solution.py:64
  146.2 2.1 %collective-permute-start.17 = (bf16[4,128,256]{2,1,0:T(8,128)(2,1)S(1)}, bf16[4,128,256]{2,1,0:T(8,128)(2,1)S(1)}, u32[]{:S(2)}, u32[]{:S(2)}) collective-permute-start(bf16[4,128,256]{2,1,0:T(8,128)(2,1)S(1)} %collective-permute-done.15), channel_id=1, source_target_pairs={{0,1},{1,2},{2,3},{3,4},{4,5},{5,6},{6,7},{7,8},{8,9},{9,10},{10,1... | collective-permute-start | bytes 786440 | tf_op jit(solution)/shard_map/ppermute | solution.py:64
  148.3 0.7 bitcast_dynamic-update-slice_fusion.2
  149.0 0.7 bitcast_dynamic-update-slice_fusion.1
  149.7 5.9 %collective-permute-done.17 = bf16[4,128,256]{2,1,0:T(8,128)(2,1)S(1)} collective-permute-done((bf16[4,128,256]{2,1,0:T(8,128)(2,1)S(1)}, bf16[4,128,256]{2,1,0:T(8,128)(2,1)S(1)}, u32[]{:S(2)}, u32[]{:S(2)}) %collective-permute-start.17) | collective-permute-done | bytes 262176 | tf_op jit(solution)/shard_map/ppermute | solution.py:64
  155.6 0.7 bitcast_dynamic-update-slice_fusion
  156.4 3.4 %fusion.13 = bf16[128,384]{1,0:T(8,128)(2,1)S(1)} fusion(bf16[128,5120]{1,0:T(8,128)(2,1)S(1)} %copy-done, bf16[5120,384]{0,1:T(8,128)(2,1)} %all-gather.2.cloned.1.call-done), kind=kOutput, calls=%fused_computation.14 | convolution fusion | flops 503414784 | bytes 5341184 | tf_op jit(solution)/shard_map/dot_general | solution.py:102
  159.8 0.1 copy.22
  159.9 8.3 %fusion.25 = (f32[3,128]{1,0:T(4,128)S(1)}, f32[3,128,8192]{2,1,0:T(8,128)}) fusion(bf16[3,128,128]{1,2,0:T(8,128)(2,1)S(1)} %bitcast.84, bf16[8192,256]{1,0:T(8,128)(2,1)} %bitcast.25, pred[128,8192]{1,0:T(8,128)(4,1)S(1)} %compare_and_fusion), kind=kOutput, calls=%fused_computation.54 | convolution fusion | flops 811597440 | bytes 15828480 | tf_op jit(solution)/shard_map/while/body/eval_jaxpr/hqd,kd->hqk/dot_general | solution.py:28
  168.2 7.6 %fusion = f32[3,128]{1,0:T(4,128)S(1)} fusion(f32[3,128,8192]{2,1,0:T(8,128)} %get-tuple-element.40, f32[3,128]{1,0:T(4,128)S(1)} %get-tuple-element.26, pred[128,8192]{1,0:T(8,128)(4,1)S(1)} %compare_and_fusion), kind=kLoop, calls=%fused_computation.2 | loop fusion | flops 9436800 | bytes 13634560 | tf_op jit(solution)/shard_map/while/body/eval_jaxpr/reduce_sum | solution.py:34
  175.8 7.9 %fusion.17 = bf16[128,3,128]{0,2,1:T(8,128)(2,1)S(1)} fusion(bf16[8192,256]{1,0:T(8,128)(2,1)} %bitcast.25, f32[3,128,8192]{2,1,0:T(8,128)} %get-tuple-element.40, f32[3,128]{1,0:T(4,128)S(1)} %get-tuple-element.26, pred[128,8192]{1,0:T(8,128)(4,1)S(1)} %compare_and_fusion, f32[128,3]{0,1:T(4,128)S(1)} %bitcast_add_fusion, f32[128,3]{0,1:T(4,128)S(1)} %get-tuple-element.25), kind=kOutput, calls=%fused_computation.16 | convolution fusion | flops 814891008 | bytes 15831552 | tf_op jit(solution)/shard_map/while/body/eval_jaxpr/hqk,kd->hqd/dot_general | solution.py:35
  183.7 0.8 copy.25
  (16 shorter events, 0.1 us)
Async XLA Ops:
  6.5 149.8 %copy-start = (bf16[128,5120]{1,0:T(8,128)(2,1)S(1)}, bf16[128,5120]{1,0:T(8,128)(2,1)}, u32[]{:S(2)}) copy-start(bf16[128,5120]{1,0:T(8,128)(2,1)} %param.7) | copy-start | bytes 3932164
  6.5 149.8 %all-gather.2.cloned.1.call-start = ((), (), s32[]{:S(2)}) async-start(), calls=%async_computation.1 | async-start | bytes 4177920 | tf_op jit(solution)/shard_map/all_gather | solution.py:91
  59.3 7.8 %collective-permute-start.1 = (bf16[128,256]{1,0:T(8,128)(2,1)S(1)}, bf16[128,256]{1,0:T(8,128)(2,1)S(1)}, u32[]{:S(2)}, u32[]{:S(2)}) collective-permute-start(bf16[128,256]{1,0:T(8,128)(2,1)S(1)} %get-tuple-element.24), channel_id=1, source_target_pairs={{0,32},{1,33},{2,34},{3,35},{4,36},{5,37},{6,38},{7,39},{8,40},{9,... | collective-permute-start | bytes 196616 | tf_op jit(solution)/shard_map/ppermute | solution.py:57
  60.6 7.4 %collective-permute-start = (bf16[128,256]{1,0:T(8,128)(2,1)S(1)}, bf16[128,256]{1,0:T(8,128)(2,1)S(1)}, u32[]{:S(2)}, u32[]{:S(2)}) collective-permute-start(bf16[128,256]{1,0:T(8,128)(2,1)S(1)} %get-tuple-element.24), channel_id=1, source_target_pairs={{0,16},{1,17},{2,18},{3,19},{4,20},{5,21},{6,22},{7,23},{8,24},{9,... | collective-permute-start | bytes 196616 | tf_op jit(solution)/shard_map/ppermute | solution.py:57
  61.9 9.1 %collective-permute-start.2 = (bf16[128,256]{1,0:T(8,128)(2,1)S(1)}, bf16[128,256]{1,0:T(8,128)(2,1)S(1)}, u32[]{:S(2)}, u32[]{:S(2)}) collective-permute-start(bf16[128,256]{1,0:T(8,128)(2,1)S(1)} %get-tuple-element.24), channel_id=1, source_target_pairs={{0,48},{1,49},{2,50},{3,51},{4,52},{5,53},{6,54},{7,55},{8,56},{9,... | collective-permute-start | bytes 196616 | tf_op jit(solution)/shard_map/ppermute | solution.py:57
  71.1 9.5 %collective-permute-start.3 = (bf16[4,128,256]{2,1,0:T(8,128)(2,1)S(1)}, bf16[4,128,256]{2,1,0:T(8,128)(2,1)S(1)}, u32[]{:S(2)}, u32[]{:S(2)}) collective-permute-start(bf16[4,128,256]{2,1,0:T(8,128)(2,1)S(1)} %pad_maximum_fusion), channel_id=1, source_target_pairs={{0,1},{1,2},{2,3},{3,4},{4,5},{5,6},{6,7},{7,8},{8,9},{9,10},{10,1... | collective-permute-start | bytes 786440 | tf_op jit(solution)/shard_map/ppermute | solution.py:64
  73.9 8.6 %collective-permute-start.4 = (bf16[4,128,256]{2,1,0:T(8,128)(2,1)S(1)}, bf16[4,128,256]{2,1,0:T(8,128)(2,1)S(1)}, u32[]{:S(2)}, u32[]{:S(2)}) collective-permute-start(bf16[4,128,256]{2,1,0:T(8,128)(2,1)S(1)} %pad_maximum_fusion), channel_id=1, source_target_pairs={{0,15},{1,0},{2,1},{3,2},{4,3},{5,4},{6,5},{7,6},{8,7},{9,8},{10,9... | collective-permute-start | bytes 786440 | tf_op jit(solution)/shard_map/ppermute | solution.py:70
  80.5 9.5 %collective-permute-start.5 = (bf16[4,128,256]{2,1,0:T(8,128)(2,1)S(1)}, bf16[4,128,256]{2,1,0:T(8,128)(2,1)S(1)}, u32[]{:S(2)}, u32[]{:S(2)}) collective-permute-start(bf16[4,128,256]{2,1,0:T(8,128)(2,1)S(1)} %collective-permute-done.3), channel_id=1, source_target_pairs={{0,1},{1,2},{2,3},{3,4},{4,5},{5,6},{6,7},{7,8},{8,9},{9,10},{10,1... | collective-permute-start | bytes 786440 | tf_op jit(solution)/shard_map/ppermute | solution.py:64
  82.5 9.5 %collective-permute-start.6 = (bf16[4,128,256]{2,1,0:T(8,128)(2,1)S(1)}, bf16[4,128,256]{2,1,0:T(8,128)(2,1)S(1)}, u32[]{:S(2)}, u32[]{:S(2)}) collective-permute-start(bf16[4,128,256]{2,1,0:T(8,128)(2,1)S(1)} %collective-permute-done.4), channel_id=1, source_target_pairs={{0,15},{1,0},{2,1},{3,2},{4,3},{5,4},{6,5},{7,6},{8,7},{9,8},{10,9... | collective-permute-start | bytes 786440 | tf_op jit(solution)/shard_map/ppermute | solution.py:70
  90.0 10.2 %collective-permute-start.7 = (bf16[4,128,256]{2,1,0:T(8,128)(2,1)S(1)}, bf16[4,128,256]{2,1,0:T(8,128)(2,1)S(1)}, u32[]{:S(2)}, u32[]{:S(2)}) collective-permute-start(bf16[4,128,256]{2,1,0:T(8,128)(2,1)S(1)} %collective-permute-done.5), channel_id=1, source_target_pairs={{0,1},{1,2},{2,3},{3,4},{4,5},{5,6},{6,7},{7,8},{8,9},{9,10},{10,1... | collective-permute-start | bytes 786440 | tf_op jit(solution)/shard_map/ppermute | solution.py:64
  91.9 10.2 %collective-permute-start.8 = (bf16[4,128,256]{2,1,0:T(8,128)(2,1)S(1)}, bf16[4,128,256]{2,1,0:T(8,128)(2,1)S(1)}, u32[]{:S(2)}, u32[]{:S(2)}) collective-permute-start(bf16[4,128,256]{2,1,0:T(8,128)(2,1)S(1)} %collective-permute-done.6), channel_id=1, source_target_pairs={{0,15},{1,0},{2,1},{3,2},{4,3},{5,4},{6,5},{7,6},{8,7},{9,8},{10,9... | collective-permute-start | bytes 786440 | tf_op jit(solution)/shard_map/ppermute | solution.py:70
  100.2 11.3 %collective-permute-start.9 = (bf16[4,128,256]{2,1,0:T(8,128)(2,1)S(1)}, bf16[4,128,256]{2,1,0:T(8,128)(2,1)S(1)}, u32[]{:S(2)}, u32[]{:S(2)}) collective-permute-start(bf16[4,128,256]{2,1,0:T(8,128)(2,1)S(1)} %collective-permute-done.7), channel_id=1, source_target_pairs={{0,1},{1,2},{2,3},{3,4},{4,5},{5,6},{6,7},{7,8},{8,9},{9,10},{10,1... | collective-permute-start | bytes 786440 | tf_op jit(solution)/shard_map/ppermute | solution.py:64
  102.1 11.4 %collective-permute-start.10 = (bf16[4,128,256]{2,1,0:T(8,128)(2,1)S(1)}, bf16[4,128,256]{2,1,0:T(8,128)(2,1)S(1)}, u32[]{:S(2)}, u32[]{:S(2)}) collective-permute-start(bf16[4,128,256]{2,1,0:T(8,128)(2,1)S(1)} %collective-permute-done.8), channel_id=1, source_target_pairs={{0,15},{1,0},{2,1},{3,2},{4,3},{5,4},{6,5},{7,6},{8,7},{9,8},{10,9... | collective-permute-start | bytes 786440 | tf_op jit(solution)/shard_map/ppermute | solution.py:70
  111.5 12.1 %collective-permute-start.11 = (bf16[4,128,256]{2,1,0:T(8,128)(2,1)S(1)}, bf16[4,128,256]{2,1,0:T(8,128)(2,1)S(1)}, u32[]{:S(2)}, u32[]{:S(2)}) collective-permute-start(bf16[4,128,256]{2,1,0:T(8,128)(2,1)S(1)} %collective-permute-done.9), channel_id=1, source_target_pairs={{0,1},{1,2},{2,3},{3,4},{4,5},{5,6},{6,7},{7,8},{8,9},{9,10},{10,1... | collective-permute-start | bytes 786440 | tf_op jit(solution)/shard_map/ppermute | solution.py:64
  113.5 12.2 %collective-permute-start.12 = (bf16[4,128,256]{2,1,0:T(8,128)(2,1)S(1)}, bf16[4,128,256]{2,1,0:T(8,128)(2,1)S(1)}, u32[]{:S(2)}, u32[]{:S(2)}) collective-permute-start(bf16[4,128,256]{2,1,0:T(8,128)(2,1)S(1)} %collective-permute-done.10), channel_id=1, source_target_pairs={{0,15},{1,0},{2,1},{3,2},{4,3},{5,4},{6,5},{7,6},{8,7},{9,8},{10,9... | collective-permute-start | bytes 786440 | tf_op jit(solution)/shard_map/ppermute | solution.py:70
  123.5 11.7 %collective-permute-start.13 = (bf16[4,128,256]{2,1,0:T(8,128)(2,1)S(1)}, bf16[4,128,256]{2,1,0:T(8,128)(2,1)S(1)}, u32[]{:S(2)}, u32[]{:S(2)}) collective-permute-start(bf16[4,128,256]{2,1,0:T(8,128)(2,1)S(1)} %collective-permute-done.11), channel_id=1, source_target_pairs={{0,1},{1,2},{2,3},{3,4},{4,5},{5,6},{6,7},{7,8},{8,9},{9,10},{10,1... | collective-permute-start | bytes 786440 | tf_op jit(solution)/shard_map/ppermute | solution.py:64
  125.7 11.5 %collective-permute-start.14 = (bf16[4,128,256]{2,1,0:T(8,128)(2,1)S(1)}, bf16[4,128,256]{2,1,0:T(8,128)(2,1)S(1)}, u32[]{:S(2)}, u32[]{:S(2)}) collective-permute-start(bf16[4,128,256]{2,1,0:T(8,128)(2,1)S(1)} %collective-permute-done.12), channel_id=1, source_target_pairs={{0,15},{1,0},{2,1},{3,2},{4,3},{5,4},{6,5},{7,6},{8,7},{9,8},{10,9... | collective-permute-start | bytes 786440 | tf_op jit(solution)/shard_map/ppermute | solution.py:70
  135.3 10.9 %collective-permute-start.15 = (bf16[4,128,256]{2,1,0:T(8,128)(2,1)S(1)}, bf16[4,128,256]{2,1,0:T(8,128)(2,1)S(1)}, u32[]{:S(2)}, u32[]{:S(2)}) collective-permute-start(bf16[4,128,256]{2,1,0:T(8,128)(2,1)S(1)} %collective-permute-done.13), channel_id=1, source_target_pairs={{0,1},{1,2},{2,3},{3,4},{4,5},{5,6},{6,7},{7,8},{8,9},{9,10},{10,1... | collective-permute-start | bytes 786440 | tf_op jit(solution)/shard_map/ppermute | solution.py:64
  137.2 11.8 %collective-permute-start.16 = (bf16[4,128,256]{2,1,0:T(8,128)(2,1)S(1)}, bf16[4,128,256]{2,1,0:T(8,128)(2,1)S(1)}, u32[]{:S(2)}, u32[]{:S(2)}) collective-permute-start(bf16[4,128,256]{2,1,0:T(8,128)(2,1)S(1)} %collective-permute-done.14), channel_id=1, source_target_pairs={{0,15},{1,0},{2,1},{3,2},{4,3},{5,4},{6,5},{7,6},{8,7},{9,8},{10,9... | collective-permute-start | bytes 786440 | tf_op jit(solution)/shard_map/ppermute | solution.py:70
  146.2 9.5 %collective-permute-start.17 = (bf16[4,128,256]{2,1,0:T(8,128)(2,1)S(1)}, bf16[4,128,256]{2,1,0:T(8,128)(2,1)S(1)}, u32[]{:S(2)}, u32[]{:S(2)}) collective-permute-start(bf16[4,128,256]{2,1,0:T(8,128)(2,1)S(1)} %collective-permute-done.15), channel_id=1, source_target_pairs={{0,1},{1,2},{2,3},{3,4},{4,5},{5,6},{6,7},{7,8},{8,9},{9,10},{10,1... | collective-permute-start | bytes 786440 | tf_op jit(solution)/shard_map/ppermute | solution.py:64
Sparse Core Ops, SparseCore 0:
  57.8 78.2 all-gather.1

commit v3 on v2

--- a/solution.py
+++ b/solution.py
@@ -3,7 +3,55 @@
 import jax
 import jax.numpy as jnp
 from jax import lax
+from jax.experimental import pallas as pl
+from jax.experimental.pallas import tpu as pltpu
 from jax.sharding import PartitionSpec as P
+
+CHUNK = 512
+
+def attn_kernel(q_ref, k_ref, v_ref, kp_ref, lo_ref, hi_ref, o_ref, s_ref):
+    n = k_ref.shape[0] // CHUNK
+    q = q_ref[...]
+    lo = lo_ref[...]
+    hi = hi_ref[...]
+
+    def first(c, top):
+        at = pl.multiple_of(c * CHUNK, CHUNK)
+        s = lax.dot_general(q, k_ref[pl.ds(at, CHUNK), :], (((1,), (1,)), ((), ())),
+                            preferred_element_type=jnp.float32)
+        kp = kp_ref[:, pl.ds(at, CHUNK)]
+        s = jnp.where((kp >= lo) & (kp <= hi), s, -1e30)
+        s_ref[:, pl.ds(at, CHUNK)] = s
+        return jnp.maximum(top, jnp.max(s, axis=1, keepdims=True))
+
+    top = lax.fori_loop(0, n, first, jnp.full((q.shape[0], 1), -1e30, jnp.float32))
+
+    def second(c, carry):
+        total, accum = carry
+        at = pl.multiple_of(c * CHUNK, CHUNK)
+        s = s_ref[:, pl.ds(at, CHUNK)]
+        kp = kp_ref[:, pl.ds(at, CHUNK)]
+        w = jnp.where((kp >= lo) & (kp <= hi), jnp.exp(s - top), 0.0)
+        total = total + jnp.sum(w, axis=1, keepdims=True)
+        accum = accum + jnp.dot(w.astype(jnp.bfloat16), v_ref[pl.ds(at, CHUNK), :],
+                                preferred_element_type=jnp.float32)
+        return total, accum
+
+    total, accum = lax.fori_loop(
+        0, n, second,
+        (jnp.zeros((q.shape[0], 1), jnp.float32), jnp.zeros((q.shape[0], v_ref.shape[1]), jnp.float32)))
+    o_ref[...] = (accum / total).astype(o_ref.dtype)
+
+
+def attend_pallas(q, keys, values, key_pos, lo, hi, interpret=False):
+    rows = q.shape[0]
+    return pl.pallas_call(
+        attn_kernel,
+        out_shape=jax.ShapeDtypeStruct((rows, values.shape[1]), jnp.bfloat16),
+        scratch_shapes=[pltpu.VMEM((rows, keys.shape[0]), jnp.float32)],
+        interpret=interpret,
+    )(q, keys, values, key_pos.reshape(1, -1), lo.reshape(-1, 1), hi.reshape(-1, 1))
+
 
 HEAD_DIM = 128
 QUERY_HEADS = 3
@@ -103,17 +151,15 @@
     queries = (projected * HEAD_DIM ** (-0.5)).astype(jnp.bfloat16)
     queries = jnp.transpose(queries.reshape(rows, QUERY_HEADS, HEAD_DIM), (1, 0, 2))
     position = lax.axis_index("ctx") * rows + jnp.arange(rows, dtype=jnp.int32)
-    attend = make_attend(queries, position, doc_start)
-    initial = (
-        jnp.full((QUERY_HEADS, rows), -1e30, jnp.float32),
-        jnp.zeros((QUERY_HEADS, rows), jnp.float32),
-        jnp.zeros((QUERY_HEADS, rows, HEAD_DIM), jnp.float32),
-    )
     width = stored_keys.shape[1]
-    top_final, total_final, accum_final = attend(
-        initial, (kv_all[:, :width], kv_all[:, width:], key_pos)
-    )
-    mixed = (accum_final / total_final[..., None]).astype(jnp.bfloat16)
+    mixed = attend_pallas(
+        queries.reshape(QUERY_HEADS * rows, HEAD_DIM),
+        kv_all[:, :width],
+        kv_all[:, width:],
+        key_pos,
+        jnp.tile(doc_start, QUERY_HEADS),
+        jnp.tile(position, QUERY_HEADS),
+    ).reshape(QUERY_HEADS, rows, HEAD_DIM)
     flat = jnp.transpose(mixed, (1, 0, 2)).reshape(rows, QUERY_HEADS * HEAD_DIM)
     return flat
 

time: 192 us -> 188 us (0.979)
  blocking collectives: 48.9 us -> 0 us
  waiting for transfers between devices: 25.9 us -> 59.8 us
  starting transfers between devices: 56.9 us -> 80.6 us
  matrix products: 19.6 us -> 3.39 us
  Pallas kernels: 0 us -> 15.5 us
  other arithmetic: 12.4 us -> 3.14 us
  local copies, waits for them, and re-layouts: 13.9 us -> 10.5 us
    all_to_all x1 -> x0, blocking collectives: 48.9 us -> none  [gather_weight(): rows = lax.all_to_all(spread, 'ctx', 0, 0, tiled=False)]
    all_to_all x0 -> x1, waiting for transfers between devices: none -> 25.5 us  [gather_weight(): rows = lax.all_to_all(spread, 'ctx', 0, 0, tiled=False)]
    all_to_all x0 -> x1, starting transfers between devices: none -> 22.8 us  [gather_weight(): rows = lax.all_to_all(spread, 'ctx', 0, 0, tiled=False)]
    dot_general x2 -> x0, matrix products: 16.2 us -> none  [the longest x1 8.3 us: step(): jnp.einsum('hqd,kd->hqk', q_set, key_block, preferred_element_type=jnp.fl...]
    pallas_call x0 -> x1, Pallas kernels: none -> 15.5 us  [attend_pallas(): pl.pallas_call(attn_kernel, out_shape=jax.ShapeDtypeStruct((rows, values....]
    ppermute x8, waiting for transfers between devices: 18.6 us -> 26.9 us  [gather_window(): lax.ppermute(fwd, 'ctx', [(c, c // z_ring * z_ring + (c % z_ring + 1) % z...]
    reduce_sum x1 -> x0, other arithmetic: 7.57 us -> none  [step(): total_new = total_old * fade + jnp.sum(weights, axis=2)]
    unnamed x16 -> x22, local copies, waits for them, and re-layouts: 10.1 us -> 2.64 us
  transfers between devices with their start and end apart: 19 -> 20, of which waited for: 13 -> 17; matrix products, arithmetic and copies ran while one was open for 8% -> 4% of each run, Pallas kernels for 0% -> 0%
where the time goes in v3:
time: 188 us; the launch traced here: 187 us
  starting transfers between devices  80.6 us (43%)
  waiting for transfers between devices  59.8 us (32%)
  Pallas kernels  15.5 us (8%)
  between operations  13.8 us (7%)
  local copies, waits for them, and re-layouts  10.5 us (6%)
  matrix products  3.39 us (2%)
  other arithmetic  3.14 us (2%)
    ppermute x7, starting transfers between devices, gather_window(): lax.ppermute(bwd, 'ctx', [(c, c // z_ring * z_ring + (c % z_ring - 1) % z...  37.7 us
    ppermute x8, waiting for transfers between devices, gather_window(): lax.ppermute(fwd, 'ctx', [(c, c // z_ring * z_ring + (c % z_ring + 1) % z...  26.9 us
    all_to_all x1, waiting for transfers between devices, gather_weight(): rows = lax.all_to_all(spread, 'ctx', 0, 0, tiled=False)  25.5 us
    all_to_all x1, starting transfers between devices, gather_weight(): rows = lax.all_to_all(spread, 'ctx', 0, 0, tiled=False)  22.8 us
    ppermute x8, starting transfers between devices, gather_window(): lax.ppermute(fwd, 'ctx', [(c, c // z_ring * z_ring + (c % z_ring + 1) % z...  16.1 us
    pallas_call x1, Pallas kernels, attend_pallas(): pl.pallas_call(attn_kernel, out_shape=jax.ShapeDtypeStruct((rows, values....  15.5 us
    ppermute x3, waiting for transfers between devices, gather_window(): stack.append(lax.ppermute(kv, 'ctx', perm))  4.68 us
    ppermute x3, starting transfers between devices, gather_window(): stack.append(lax.ppermute(kv, 'ctx', perm))  3.88 us
  transfers between devices with their start and end apart: 20, of which 17 were waited for; matrix products, arithmetic and copies ran while one was open for 4% of the time, Pallas kernels for 0%

profile of v3, /device:TPU:26, one launch (start us, length us, event | category | flops | bytes accessed | tf_op | source)
XLA Modules:
  0.0 186.8 jit_solution(18339281612698644478)
XLA Ops:
  6.5 0.0 copy-start
  6.5 1.6 broadcast_in_dim.14
  8.1 22.8 %all-to-all-start = ((bf16[64,80,24]{1,2,0:T(8,128)(2,1)}), bf16[64,80,24]{1,2,0:T(8,128)(2,1)S(1)}, u32[]{:S(2)}, u32[]{:S(2)}) async-start(bf16[64,80,24]{1,2,0:T(8,128)(2,1)} %broadcast_in_dim.14), calls=%async_computation | async-start | bytes 786432 | tf_op jit(solution)/shard_map/all_to_all | solution.py:137
  30.9 0.0 all-gather.2.cloned.1.call-start
  31.0 0.7 bitcast_convert_fusion.1
  31.7 25.5 %all-to-all-done = bf16[64,80,24]{1,2,0:T(8,128)(2,1)S(1)} async-done(((bf16[64,80,24]{1,2,0:T(8,128)(2,1)}), bf16[64,80,24]{1,2,0:T(8,128)(2,1)S(1)}, u32[]{:S(2)}, u32[]{:S(2)}) %all-to-all-start) | async-done | bytes 245792 | tf_op jit(solution)/shard_map/all_to_all | solution.py:137
  57.2 0.1 copy.24
  57.3 1.3 reshape.103
  58.6 0.0 all-gather.2.cloned.1.call-update
  58.6 0.9 multiply_convert_fusion
  59.5 1.3 collective-permute-start
  60.8 1.3 collective-permute-start.1
  62.1 1.3 collective-permute-start.2
  63.5 0.8 copy.34
  64.3 0.7 broadcast_bitcast_fusion.1
  65.0 0.8 copy.32
  65.8 0.7 and_select_fusion
  66.5 0.1 add_multiply_fusion
  66.6 0.0 collective-permute-done
  66.6 1.9 %collective-permute-done.1 = bf16[128,256]{1,0:T(8,128)(2,1)S(1)} collective-permute-done((bf16[128,256]{1,0:T(8,128)(2,1)S(1)}, bf16[128,256]{1,0:T(8,128)(2,1)S(1)}, u32[]{:S(2)}, u32[]{:S(2)}) %collective-permute-start.1) | collective-permute-done | bytes 65568 | tf_op jit(solution)/shard_map/ppermute | solution.py:105
  68.5 2.8 %collective-permute-done.2 = bf16[128,256]{1,0:T(8,128)(2,1)S(1)} collective-permute-done((bf16[128,256]{1,0:T(8,128)(2,1)S(1)}, bf16[128,256]{1,0:T(8,128)(2,1)S(1)}, u32[]{:S(2)}, u32[]{:S(2)}) %collective-permute-start.2) | collective-permute-done | bytes 65568 | tf_op jit(solution)/shard_map/ppermute | solution.py:105
  71.3 2.8 %collective-permute-start.3 = (bf16[4,128,256]{2,1,0:T(8,128)(2,1)S(1)}, bf16[4,128,256]{2,1,0:T(8,128)(2,1)S(1)}, u32[]{:S(2)}, u32[]{:S(2)}) collective-permute-start(bf16[4,128,256]{2,1,0:T(8,128)(2,1)S(1)} %pad_maximum_fusion), channel_id=1, source_target_pairs={{0,1},{1,2},{2,3},{3,4},{4,5},{5,6},{6,7},{7,8},{8,9},{9,10},{10,1... | collective-permute-start | bytes 786440 | tf_op jit(solution)/shard_map/ppermute | solution.py:112
  74.1 0.7 add_select_fusion
  74.8 4.3 %collective-permute-start.4 = (bf16[4,128,256]{2,1,0:T(8,128)(2,1)S(1)}, bf16[4,128,256]{2,1,0:T(8,128)(2,1)S(1)}, u32[]{:S(2)}, u32[]{:S(2)}) collective-permute-start(bf16[4,128,256]{2,1,0:T(8,128)(2,1)S(1)} %pad_maximum_fusion), channel_id=1, source_target_pairs={{0,15},{1,0},{2,1},{3,2},{4,3},{5,4},{6,5},{7,6},{8,7},{9,8},{10,9... | collective-permute-start | bytes 786440 | tf_op jit(solution)/shard_map/ppermute | solution.py:118
  79.1 1.7 collective-permute-done.3
  80.8 1.9 %collective-permute-start.5 = (bf16[4,128,256]{2,1,0:T(8,128)(2,1)S(1)}, bf16[4,128,256]{2,1,0:T(8,128)(2,1)S(1)}, u32[]{:S(2)}, u32[]{:S(2)}) collective-permute-start(bf16[4,128,256]{2,1,0:T(8,128)(2,1)S(1)} %collective-permute-done.3), channel_id=1, source_target_pairs={{0,1},{1,2},{2,3},{3,4},{4,5},{5,6},{6,7},{7,8},{8,9},{9,10},{10,1... | collective-permute-start | bytes 786440 | tf_op jit(solution)/shard_map/ppermute | solution.py:112
  82.7 0.3 collective-permute-done.4
  83.1 5.5 %collective-permute-start.6 = (bf16[4,128,256]{2,1,0:T(8,128)(2,1)S(1)}, bf16[4,128,256]{2,1,0:T(8,128)(2,1)S(1)}, u32[]{:S(2)}, u32[]{:S(2)}) collective-permute-start(bf16[4,128,256]{2,1,0:T(8,128)(2,1)S(1)} %collective-permute-done.4), channel_id=1, source_target_pairs={{0,15},{1,0},{2,1},{3,2},{4,3},{5,4},{6,5},{7,6},{8,7},{9,8},{10,9... | collective-permute-start | bytes 786440 | tf_op jit(solution)/shard_map/ppermute | solution.py:118
  88.6 1.7 collective-permute-done.5
  90.3 1.9 %collective-permute-start.7 = (bf16[4,128,256]{2,1,0:T(8,128)(2,1)S(1)}, bf16[4,128,256]{2,1,0:T(8,128)(2,1)S(1)}, u32[]{:S(2)}, u32[]{:S(2)}) collective-permute-start(bf16[4,128,256]{2,1,0:T(8,128)(2,1)S(1)} %collective-permute-done.5), channel_id=1, source_target_pairs={{0,1},{1,2},{2,3},{3,4},{4,5},{5,6},{6,7},{7,8},{8,9},{9,10},{10,1... | collective-permute-start | bytes 786440 | tf_op jit(solution)/shard_map/ppermute | solution.py:112
  92.2 0.2 collective-permute-done.6
  92.4 5.7 %collective-permute-start.8 = (bf16[4,128,256]{2,1,0:T(8,128)(2,1)S(1)}, bf16[4,128,256]{2,1,0:T(8,128)(2,1)S(1)}, u32[]{:S(2)}, u32[]{:S(2)}) collective-permute-start(bf16[4,128,256]{2,1,0:T(8,128)(2,1)S(1)} %collective-permute-done.6), channel_id=1, source_target_pairs={{0,15},{1,0},{2,1},{3,2},{4,3},{5,4},{6,5},{7,6},{8,7},{9,8},{10,9... | collective-permute-start | bytes 786440 | tf_op jit(solution)/shard_map/ppermute | solution.py:118
  98.1 2.6 %collective-permute-done.7 = bf16[4,128,256]{2,1,0:T(8,128)(2,1)S(1)} collective-permute-done((bf16[4,128,256]{2,1,0:T(8,128)(2,1)S(1)}, bf16[4,128,256]{2,1,0:T(8,128)(2,1)S(1)}, u32[]{:S(2)}, u32[]{:S(2)}) %collective-permute-start.7) | collective-permute-done | bytes 262176 | tf_op jit(solution)/shard_map/ppermute | solution.py:112
  100.7 1.9 %collective-permute-start.9 = (bf16[4,128,256]{2,1,0:T(8,128)(2,1)S(1)}, bf16[4,128,256]{2,1,0:T(8,128)(2,1)S(1)}, u32[]{:S(2)}, u32[]{:S(2)}) collective-permute-start(bf16[4,128,256]{2,1,0:T(8,128)(2,1)S(1)} %collective-permute-done.7), channel_id=1, source_target_pairs={{0,1},{1,2},{2,3},{3,4},{4,5},{5,6},{6,7},{7,8},{8,9},{9,10},{10,1... | collective-permute-start | bytes 786440 | tf_op jit(solution)/shard_map/ppermute | solution.py:112
  102.6 0.6 collective-permute-done.8
  103.2 5.6 %collective-permute-start.10 = (bf16[4,128,256]{2,1,0:T(8,128)(2,1)S(1)}, bf16[4,128,256]{2,1,0:T(8,128)(2,1)S(1)}, u32[]{:S(2)}, u32[]{:S(2)}) collective-permute-start(bf16[4,128,256]{2,1,0:T(8,128)(2,1)S(1)} %collective-permute-done.8), channel_id=1, source_target_pairs={{0,15},{1,0},{2,1},{3,2},{4,3},{5,4},{6,5},{7,6},{8,7},{9,8},{10,9... | collective-permute-start | bytes 786440 | tf_op jit(solution)/shard_map/ppermute | solution.py:118
  108.8 3.4 %collective-permute-done.9 = bf16[4,128,256]{2,1,0:T(8,128)(2,1)S(1)} collective-permute-done((bf16[4,128,256]{2,1,0:T(8,128)(2,1)S(1)}, bf16[4,128,256]{2,1,0:T(8,128)(2,1)S(1)}, u32[]{:S(2)}, u32[]{:S(2)}) %collective-permute-start.9) | collective-permute-done | bytes 262176 | tf_op jit(solution)/shard_map/ppermute | solution.py:112
  112.2 1.9 %collective-permute-start.11 = (bf16[4,128,256]{2,1,0:T(8,128)(2,1)S(1)}, bf16[4,128,256]{2,1,0:T(8,128)(2,1)S(1)}, u32[]{:S(2)}, u32[]{:S(2)}) collective-permute-start(bf16[4,128,256]{2,1,0:T(8,128)(2,1)S(1)} %collective-permute-done.9), channel_id=1, source_target_pairs={{0,1},{1,2},{2,3},{3,4},{4,5},{5,6},{6,7},{7,8},{8,9},{9,10},{10,1... | collective-permute-start | bytes 786440 | tf_op jit(solution)/shard_map/ppermute | solution.py:112
  114.2 0.8 collective-permute-done.10
  115.0 5.6 %collective-permute-start.12 = (bf16[4,128,256]{2,1,0:T(8,128)(2,1)S(1)}, bf16[4,128,256]{2,1,0:T(8,128)(2,1)S(1)}, u32[]{:S(2)}, u32[]{:S(2)}) collective-permute-start(bf16[4,128,256]{2,1,0:T(8,128)(2,1)S(1)} %collective-permute-done.10), channel_id=1, source_target_pairs={{0,15},{1,0},{2,1},{3,2},{4,3},{5,4},{6,5},{7,6},{8,7},{9,8},{10,9... | collective-permute-start | bytes 786440 | tf_op jit(solution)/shard_map/ppermute | solution.py:118
  120.6 3.9 %collective-permute-done.11 = bf16[4,128,256]{2,1,0:T(8,128)(2,1)S(1)} collective-permute-done((bf16[4,128,256]{2,1,0:T(8,128)(2,1)S(1)}, bf16[4,128,256]{2,1,0:T(8,128)(2,1)S(1)}, u32[]{:S(2)}, u32[]{:S(2)}) %collective-permute-start.11) | collective-permute-done | bytes 262176 | tf_op jit(solution)/shard_map/ppermute | solution.py:112
  124.5 1.9 %collective-permute-start.13 = (bf16[4,128,256]{2,1,0:T(8,128)(2,1)S(1)}, bf16[4,128,256]{2,1,0:T(8,128)(2,1)S(1)}, u32[]{:S(2)}, u32[]{:S(2)}) collective-permute-start(bf16[4,128,256]{2,1,0:T(8,128)(2,1)S(1)} %collective-permute-done.11), channel_id=1, source_target_pairs={{0,1},{1,2},{2,3},{3,4},{4,5},{5,6},{6,7},{7,8},{8,9},{9,10},{10,1... | collective-permute-start | bytes 786440 | tf_op jit(solution)/shard_map/ppermute | solution.py:112
  126.4 0.6 collective-permute-done.12
  127.0 5.6 %collective-permute-start.14 = (bf16[4,128,256]{2,1,0:T(8,128)(2,1)S(1)}, bf16[4,128,256]{2,1,0:T(8,128)(2,1)S(1)}, u32[]{:S(2)}, u32[]{:S(2)}) collective-permute-start(bf16[4,128,256]{2,1,0:T(8,128)(2,1)S(1)} %collective-permute-done.12), channel_id=1, source_target_pairs={{0,15},{1,0},{2,1},{3,2},{4,3},{5,4},{6,5},{7,6},{8,7},{9,8},{10,9... | collective-permute-start | bytes 786440 | tf_op jit(solution)/shard_map/ppermute | solution.py:118
  132.6 3.4 %collective-permute-done.13 = bf16[4,128,256]{2,1,0:T(8,128)(2,1)S(1)} collective-permute-done((bf16[4,128,256]{2,1,0:T(8,128)(2,1)S(1)}, bf16[4,128,256]{2,1,0:T(8,128)(2,1)S(1)}, u32[]{:S(2)}, u32[]{:S(2)}) %collective-permute-start.13) | collective-permute-done | bytes 262176 | tf_op jit(solution)/shard_map/ppermute | solution.py:112
  136.0 1.9 %collective-permute-start.15 = (bf16[4,128,256]{2,1,0:T(8,128)(2,1)S(1)}, bf16[4,128,256]{2,1,0:T(8,128)(2,1)S(1)}, u32[]{:S(2)}, u32[]{:S(2)}) collective-permute-start(bf16[4,128,256]{2,1,0:T(8,128)(2,1)S(1)} %collective-permute-done.13), channel_id=1, source_target_pairs={{0,1},{1,2},{2,3},{3,4},{4,5},{5,6},{6,7},{7,8},{8,9},{9,10},{10,1... | collective-permute-start | bytes 786440 | tf_op jit(solution)/shard_map/ppermute | solution.py:112
  137.9 0.3 collective-permute-done.14
  138.2 5.6 %collective-permute-start.16 = (bf16[4,128,256]{2,1,0:T(8,128)(2,1)S(1)}, bf16[4,128,256]{2,1,0:T(8,128)(2,1)S(1)}, u32[]{:S(2)}, u32[]{:S(2)}) collective-permute-start(bf16[4,128,256]{2,1,0:T(8,128)(2,1)S(1)} %collective-permute-done.14), channel_id=1, source_target_pairs={{0,15},{1,0},{2,1},{3,2},{4,3},{5,4},{6,5},{7,6},{8,7},{9,8},{10,9... | collective-permute-start | bytes 786440 | tf_op jit(solution)/shard_map/ppermute | solution.py:118
  143.8 2.8 %collective-permute-done.15 = bf16[4,128,256]{2,1,0:T(8,128)(2,1)S(1)} collective-permute-done((bf16[4,128,256]{2,1,0:T(8,128)(2,1)S(1)}, bf16[4,128,256]{2,1,0:T(8,128)(2,1)S(1)}, u32[]{:S(2)}, u32[]{:S(2)}) %collective-permute-start.15) | collective-permute-done | bytes 262176 | tf_op jit(solution)/shard_map/ppermute | solution.py:112
  146.6 1.9 %collective-permute-start.17 = (bf16[4,128,256]{2,1,0:T(8,128)(2,1)S(1)}, bf16[4,128,256]{2,1,0:T(8,128)(2,1)S(1)}, u32[]{:S(2)}, u32[]{:S(2)}) collective-permute-start(bf16[4,128,256]{2,1,0:T(8,128)(2,1)S(1)} %collective-permute-done.15), channel_id=1, source_target_pairs={{0,1},{1,2},{2,3},{3,4},{4,5},{5,6},{6,7},{7,8},{8,9},{9,10},{10,1... | collective-permute-start | bytes 786440 | tf_op jit(solution)/shard_map/ppermute | solution.py:112
  148.5 0.0 collective-permute-done.16
  148.6 7.5 %collective-permute-done.17 = bf16[4,128,256]{2,1,0:T(8,128)(2,1)S(1)} collective-permute-done((bf16[4,128,256]{2,1,0:T(8,128)(2,1)S(1)}, bf16[4,128,256]{2,1,0:T(8,128)(2,1)S(1)}, u32[]{:S(2)}, u32[]{:S(2)}) %collective-permute-start.17) | collective-permute-done | bytes 262176 | tf_op jit(solution)/shard_map/ppermute | solution.py:112
  156.1 2.2 %fusion.5 = (bf16[8192,128]{1,0:T(8,128)(2,1)}, bf16[8192,128]{1,0:T(8,128)(2,1)}) fusion(bf16[8192,256]{1,0:T(8,128)(2,1)S(1)} %bitcast.71), kind=kLoop, calls=%fused_computation.39 | loop fusion | bytes 8388608 | tf_op jit(solution)/shard_map/slice | solution.py:158
  158.3 0.0 all-gather.2.cloned.1.call-done
  158.3 0.0 copy-done
  158.3 3.4 %fusion = bf16[128,384]{1,0:T(8,128)(2,1)S(1)} fusion(bf16[128,5120]{1,0:T(8,128)(2,1)S(1)} %copy-done, bf16[5120,384]{0,1:T(8,128)(2,1)} %all-gather.2.cloned.1.call-done), kind=kOutput, calls=%fused_computation.1 | convolution fusion | flops 503414784 | bytes 5341184 | tf_op jit(solution)/shard_map/dot_general | solution.py:150
  161.7 0.1 copy.25
  161.8 0.8 copy.26
  162.6 15.5 %shard_map.73 = bf16[384,128]{1,0:T(8,128)(2,1)} custom-call(bf16[384,128]{1,0:T(8,128)(2,1)} %bitcast.76, bf16[8192,128]{1,0:T(8,128)(2,1)} %get-tuple-element.6.k_ref, bf16[8192,128]{1,0:T(8,128)(2,1)} %get-tuple-element.5.v_ref, s32[1,8192]{1,0:T(1,128)} %bitcast.84, s32[384,1]{1,0:T(8,128)} %bitcast.73, s32[384,1]{1,0:T(8,128)} %bitcast.72), custom_call_target="tpu_custom_call" | custom-call | tf_op jit(solution)/shard_map/pallas_call | solution.py:48
  178.1 1.0 copy.29
  179.2 0.8 copy.30
  (24 shorter events, 0.4 us)
Async XLA Ops:
  6.5 151.8 %copy-start = (bf16[128,5120]{1,0:T(8,128)(2,1)S(1)}, bf16[128,5120]{1,0:T(8,128)(2,1)}, u32[]{:S(2)}) copy-start(bf16[128,5120]{1,0:T(8,128)(2,1)} %param.7) | copy-start | bytes 3932164
  8.1 49.1 %all-to-all-start = ((bf16[64,80,24]{1,2,0:T(8,128)(2,1)}), bf16[64,80,24]{1,2,0:T(8,128)(2,1)S(1)}, u32[]{:S(2)}, u32[]{:S(2)}) async-start(bf16[64,80,24]{1,2,0:T(8,128)(2,1)} %broadcast_in_dim.14), calls=%async_computation | async-start | bytes 786432 | tf_op jit(solution)/shard_map/all_to_all | solution.py:137
  30.9 127.4 %all-gather.2.cloned.1.call-start = ((), (), s32[]{:S(2)}) async-start(), calls=%async_computation.1 | async-start | bytes 4177920 | tf_op jit(solution)/shard_map/all_gather | solution.py:139
  59.5 7.1 %collective-permute-start = (bf16[128,256]{1,0:T(8,128)(2,1)S(1)}, bf16[128,256]{1,0:T(8,128)(2,1)S(1)}, u32[]{:S(2)}, u32[]{:S(2)}) collective-permute-start(bf16[128,256]{1,0:T(8,128)(2,1)S(1)} %get-tuple-element.8), channel_id=1, source_target_pairs={{0,16},{1,17},{2,18},{3,19},{4,20},{5,21},{6,22},{7,23},{8,24},{9,... | collective-permute-start | bytes 196616 | tf_op jit(solution)/shard_map/ppermute | solution.py:105
  60.8 7.7 %collective-permute-start.1 = (bf16[128,256]{1,0:T(8,128)(2,1)S(1)}, bf16[128,256]{1,0:T(8,128)(2,1)S(1)}, u32[]{:S(2)}, u32[]{:S(2)}) collective-permute-start(bf16[128,256]{1,0:T(8,128)(2,1)S(1)} %get-tuple-element.8), channel_id=1, source_target_pairs={{0,32},{1,33},{2,34},{3,35},{4,36},{5,37},{6,38},{7,39},{8,40},{9,... | collective-permute-start | bytes 196616 | tf_op jit(solution)/shard_map/ppermute | solution.py:105
  62.1 9.1 %collective-permute-start.2 = (bf16[128,256]{1,0:T(8,128)(2,1)S(1)}, bf16[128,256]{1,0:T(8,128)(2,1)S(1)}, u32[]{:S(2)}, u32[]{:S(2)}) collective-permute-start(bf16[128,256]{1,0:T(8,128)(2,1)S(1)} %get-tuple-element.8), channel_id=1, source_target_pairs={{0,48},{1,49},{2,50},{3,51},{4,52},{5,53},{6,54},{7,55},{8,56},{9,... | collective-permute-start | bytes 196616 | tf_op jit(solution)/shard_map/ppermute | solution.py:105
  71.3 9.5 %collective-permute-start.3 = (bf16[4,128,256]{2,1,0:T(8,128)(2,1)S(1)}, bf16[4,128,256]{2,1,0:T(8,128)(2,1)S(1)}, u32[]{:S(2)}, u32[]{:S(2)}) collective-permute-start(bf16[4,128,256]{2,1,0:T(8,128)(2,1)S(1)} %pad_maximum_fusion), channel_id=1, source_target_pairs={{0,1},{1,2},{2,3},{3,4},{4,5},{5,6},{6,7},{7,8},{8,9},{9,10},{10,1... | collective-permute-start | bytes 786440 | tf_op jit(solution)/shard_map/ppermute | solution.py:112
  74.8 8.3 %collective-permute-start.4 = (bf16[4,128,256]{2,1,0:T(8,128)(2,1)S(1)}, bf16[4,128,256]{2,1,0:T(8,128)(2,1)S(1)}, u32[]{:S(2)}, u32[]{:S(2)}) collective-permute-start(bf16[4,128,256]{2,1,0:T(8,128)(2,1)S(1)} %pad_maximum_fusion), channel_id=1, source_target_pairs={{0,15},{1,0},{2,1},{3,2},{4,3},{5,4},{6,5},{7,6},{8,7},{9,8},{10,9... | collective-permute-start | bytes 786440 | tf_op jit(solution)/shard_map/ppermute | solution.py:118
  80.8 9.5 %collective-permute-start.5 = (bf16[4,128,256]{2,1,0:T(8,128)(2,1)S(1)}, bf16[4,128,256]{2,1,0:T(8,128)(2,1)S(1)}, u32[]{:S(2)}, u32[]{:S(2)}) collective-permute-start(bf16[4,128,256]{2,1,0:T(8,128)(2,1)S(1)} %collective-permute-done.3), channel_id=1, source_target_pairs={{0,1},{1,2},{2,3},{3,4},{4,5},{5,6},{6,7},{7,8},{8,9},{9,10},{10,1... | collective-permute-start | bytes 786440 | tf_op jit(solution)/shard_map/ppermute | solution.py:112
  83.1 9.3 %collective-permute-start.6 = (bf16[4,128,256]{2,1,0:T(8,128)(2,1)S(1)}, bf16[4,128,256]{2,1,0:T(8,128)(2,1)S(1)}, u32[]{:S(2)}, u32[]{:S(2)}) collective-permute-start(bf16[4,128,256]{2,1,0:T(8,128)(2,1)S(1)} %collective-permute-done.4), channel_id=1, source_target_pairs={{0,15},{1,0},{2,1},{3,2},{4,3},{5,4},{6,5},{7,6},{8,7},{9,8},{10,9... | collective-permute-start | bytes 786440 | tf_op jit(solution)/shard_map/ppermute | solution.py:118
  90.3 10.4 %collective-permute-start.7 = (bf16[4,128,256]{2,1,0:T(8,128)(2,1)S(1)}, bf16[4,128,256]{2,1,0:T(8,128)(2,1)S(1)}, u32[]{:S(2)}, u32[]{:S(2)}) collective-permute-start(bf16[4,128,256]{2,1,0:T(8,128)(2,1)S(1)} %collective-permute-done.5), channel_id=1, source_target_pairs={{0,1},{1,2},{2,3},{3,4},{4,5},{5,6},{6,7},{7,8},{8,9},{9,10},{10,1... | collective-permute-start | bytes 786440 | tf_op jit(solution)/shard_map/ppermute | solution.py:112
  92.4 10.7 %collective-permute-start.8 = (bf16[4,128,256]{2,1,0:T(8,128)(2,1)S(1)}, bf16[4,128,256]{2,1,0:T(8,128)(2,1)S(1)}, u32[]{:S(2)}, u32[]{:S(2)}) collective-permute-start(bf16[4,128,256]{2,1,0:T(8,128)(2,1)S(1)} %collective-permute-done.6), channel_id=1, source_target_pairs={{0,15},{1,0},{2,1},{3,2},{4,3},{5,4},{6,5},{7,6},{8,7},{9,8},{10,9... | collective-permute-start | bytes 786440 | tf_op jit(solution)/shard_map/ppermute | solution.py:118
  100.7 11.5 %collective-permute-start.9 = (bf16[4,128,256]{2,1,0:T(8,128)(2,1)S(1)}, bf16[4,128,256]{2,1,0:T(8,128)(2,1)S(1)}, u32[]{:S(2)}, u32[]{:S(2)}) collective-permute-start(bf16[4,128,256]{2,1,0:T(8,128)(2,1)S(1)} %collective-permute-done.7), channel_id=1, source_target_pairs={{0,1},{1,2},{2,3},{3,4},{4,5},{5,6},{6,7},{7,8},{8,9},{9,10},{10,1... | collective-permute-start | bytes 786440 | tf_op jit(solution)/shard_map/ppermute | solution.py:112
  103.2 11.8 %collective-permute-start.10 = (bf16[4,128,256]{2,1,0:T(8,128)(2,1)S(1)}, bf16[4,128,256]{2,1,0:T(8,128)(2,1)S(1)}, u32[]{:S(2)}, u32[]{:S(2)}) collective-permute-start(bf16[4,128,256]{2,1,0:T(8,128)(2,1)S(1)} %collective-permute-done.8), channel_id=1, source_target_pairs={{0,15},{1,0},{2,1},{3,2},{4,3},{5,4},{6,5},{7,6},{8,7},{9,8},{10,9... | collective-permute-start | bytes 786440 | tf_op jit(solution)/shard_map/ppermute | solution.py:118
  112.2 12.2 %collective-permute-start.11 = (bf16[4,128,256]{2,1,0:T(8,128)(2,1)S(1)}, bf16[4,128,256]{2,1,0:T(8,128)(2,1)S(1)}, u32[]{:S(2)}, u32[]{:S(2)}) collective-permute-start(bf16[4,128,256]{2,1,0:T(8,128)(2,1)S(1)} %collective-permute-done.9), channel_id=1, source_target_pairs={{0,1},{1,2},{2,3},{3,4},{4,5},{5,6},{6,7},{7,8},{8,9},{9,10},{10,1... | collective-permute-start | bytes 786440 | tf_op jit(solution)/shard_map/ppermute | solution.py:112
  115.0 12.0 %collective-permute-start.12 = (bf16[4,128,256]{2,1,0:T(8,128)(2,1)S(1)}, bf16[4,128,256]{2,1,0:T(8,128)(2,1)S(1)}, u32[]{:S(2)}, u32[]{:S(2)}) collective-permute-start(bf16[4,128,256]{2,1,0:T(8,128)(2,1)S(1)} %collective-permute-done.10), channel_id=1, source_target_pairs={{0,15},{1,0},{2,1},{3,2},{4,3},{5,4},{6,5},{7,6},{8,7},{9,8},{10,9... | collective-permute-start | bytes 786440 | tf_op jit(solution)/shard_map/ppermute | solution.py:118
  124.5 11.5 %collective-permute-start.13 = (bf16[4,128,256]{2,1,0:T(8,128)(2,1)S(1)}, bf16[4,128,256]{2,1,0:T(8,128)(2,1)S(1)}, u32[]{:S(2)}, u32[]{:S(2)}) collective-permute-start(bf16[4,128,256]{2,1,0:T(8,128)(2,1)S(1)} %collective-permute-done.11), channel_id=1, source_target_pairs={{0,1},{1,2},{2,3},{3,4},{4,5},{5,6},{6,7},{7,8},{8,9},{9,10},{10,1... | collective-permute-start | bytes 786440 | tf_op jit(solution)/shard_map/ppermute | solution.py:112
  127.0 11.2 %collective-permute-start.14 = (bf16[4,128,256]{2,1,0:T(8,128)(2,1)S(1)}, bf16[4,128,256]{2,1,0:T(8,128)(2,1)S(1)}, u32[]{:S(2)}, u32[]{:S(2)}) collective-permute-start(bf16[4,128,256]{2,1,0:T(8,128)(2,1)S(1)} %collective-permute-done.12), channel_id=1, source_target_pairs={{0,15},{1,0},{2,1},{3,2},{4,3},{5,4},{6,5},{7,6},{8,7},{9,8},{10,9... | collective-permute-start | bytes 786440 | tf_op jit(solution)/shard_map/ppermute | solution.py:118
  136.0 10.6 %collective-permute-start.15 = (bf16[4,128,256]{2,1,0:T(8,128)(2,1)S(1)}, bf16[4,128,256]{2,1,0:T(8,128)(2,1)S(1)}, u32[]{:S(2)}, u32[]{:S(2)}) collective-permute-start(bf16[4,128,256]{2,1,0:T(8,128)(2,1)S(1)} %collective-permute-done.13), channel_id=1, source_target_pairs={{0,1},{1,2},{2,3},{3,4},{4,5},{5,6},{6,7},{7,8},{8,9},{9,10},{10,1... | collective-permute-start | bytes 786440 | tf_op jit(solution)/shard_map/ppermute | solution.py:112
  138.2 10.4 %collective-permute-start.16 = (bf16[4,128,256]{2,1,0:T(8,128)(2,1)S(1)}, bf16[4,128,256]{2,1,0:T(8,128)(2,1)S(1)}, u32[]{:S(2)}, u32[]{:S(2)}) collective-permute-start(bf16[4,128,256]{2,1,0:T(8,128)(2,1)S(1)} %collective-permute-done.14), channel_id=1, source_target_pairs={{0,15},{1,0},{2,1},{3,2},{4,3},{5,4},{6,5},{7,6},{8,7},{9,8},{10,9... | collective-permute-start | bytes 786440 | tf_op jit(solution)/shard_map/ppermute | solution.py:118
  146.6 9.5 %collective-permute-start.17 = (bf16[4,128,256]{2,1,0:T(8,128)(2,1)S(1)}, bf16[4,128,256]{2,1,0:T(8,128)(2,1)S(1)}, u32[]{:S(2)}, u32[]{:S(2)}) collective-permute-start(bf16[4,128,256]{2,1,0:T(8,128)(2,1)S(1)} %collective-permute-done.15), channel_id=1, source_target_pairs={{0,1},{1,2},{2,3},{3,4},{4,5},{5,6},{6,7},{7,8},{8,9},{9,10},{10,1... | collective-permute-start | bytes 786440 | tf_op jit(solution)/shard_map/ppermute | solution.py:112
Sparse Core Ops, SparseCore 0:
  58.8 78.2 all-gather.1

commit v4 on v3

--- a/solution.py
+++ b/solution.py
@@ -9,13 +9,19 @@
 
 CHUNK = 512
 
-def attn_kernel(q_ref, k_ref, v_ref, kp_ref, lo_ref, hi_ref, o_ref, s_ref):
+def attn_kernel(kmin_ref, kmax_ref, bound_ref, q_ref, k_ref, v_ref, kp_ref, lo_ref, hi_ref, o_ref, s_ref):
     n = k_ref.shape[0] // CHUNK
     q = q_ref[...]
     lo = lo_ref[...]
     hi = hi_ref[...]
 
+    def live(c):
+        return (kmin_ref[c] <= bound_ref[1]) & (kmax_ref[c] >= bound_ref[0])
+
     def first(c, top):
+        return lax.cond(live(c), lambda: first_live(c, top), lambda: top)
+
+    def first_live(c, top):
         at = pl.multiple_of(c * CHUNK, CHUNK)
         s = lax.dot_general(q, k_ref[pl.ds(at, CHUNK), :], (((1,), (1,)), ((), ())),
                             preferred_element_type=jnp.float32)
@@ -27,6 +33,9 @@
     top = lax.fori_loop(0, n, first, jnp.full((q.shape[0], 1), -1e30, jnp.float32))
 
     def second(c, carry):
+        return lax.cond(live(c), lambda: second_live(c, carry), lambda: carry)
+
+    def second_live(c, carry):
         total, accum = carry
         at = pl.multiple_of(c * CHUNK, CHUNK)
         s = s_ref[:, pl.ds(at, CHUNK)]
@@ -45,12 +54,20 @@
 
 def attend_pallas(q, keys, values, key_pos, lo, hi, interpret=False):
     rows = q.shape[0]
+    chunks = key_pos.reshape(-1, CHUNK)
+    kmin = jnp.min(chunks, axis=1)
+    kmax = jnp.max(jnp.where(chunks < (1 << 23), chunks, -1), axis=1)
+    bound = jnp.stack([jnp.min(lo), jnp.max(hi)])
+    smem = pl.BlockSpec(memory_space=pltpu.SMEM)
+    vmem = pl.BlockSpec(memory_space=pltpu.VMEM)
     return pl.pallas_call(
         attn_kernel,
         out_shape=jax.ShapeDtypeStruct((rows, values.shape[1]), jnp.bfloat16),
         scratch_shapes=[pltpu.VMEM((rows, keys.shape[0]), jnp.float32)],
+        in_specs=[smem, smem, smem, vmem, vmem, vmem, vmem, vmem, vmem],
+        out_specs=vmem,
         interpret=interpret,
-    )(q, keys, values, key_pos.reshape(1, -1), lo.reshape(-1, 1), hi.reshape(-1, 1))
+    )(kmin, kmax, bound, q, keys, values, key_pos.reshape(1, -1), lo.reshape(-1, 1), hi.reshape(-1, 1))
 
 
 HEAD_DIM = 128

time: 188 us -> 190 us (1.011)
  the two profiles are of different devices: /device:TPU:26 before, /device:TPU:20 now
where the time goes in v4:
time: 190 us; the launch traced here: 189 us
  starting transfers between devices  82.7 us (44%)
  waiting for transfers between devices  54.2 us (29%)
  Pallas kernels  17.3 us (9%)
  between operations  13.8 us (7%)
  local copies, waits for them, and re-layouts  9.82 us (5%)
  other arithmetic  7.45 us (4%)
  matrix products  3.39 us (2%)
    ppermute x7, starting transfers between devices, gather_window(): lax.ppermute(bwd, 'ctx', [(c, c // z_ring * z_ring + (c % z_ring - 1) % z...  37.7 us
    all_to_all x1, waiting for transfers between devices, gather_weight(): rows = lax.all_to_all(spread, 'ctx', 0, 0, tiled=False)  24.6 us
    all_to_all x1, starting transfers between devices, gather_weight(): rows = lax.all_to_all(spread, 'ctx', 0, 0, tiled=False)  22.8 us
    ppermute x7, waiting for transfers between devices, gather_window(): lax.ppermute(bwd, 'ctx', [(c, c // z_ring * z_ring + (c % z_ring - 1) % z...  20.3 us
    pallas_call x1, Pallas kernels, attend_pallas(): pl.pallas_call(attn_kernel, out_shape=jax.ShapeDtypeStruct((rows, values....  17.3 us
    ppermute x8, starting transfers between devices, gather_window(): lax.ppermute(fwd, 'ctx', [(c, c // z_ring * z_ring + (c % z_ring + 1) % z...  16.2 us
    ppermute x8, waiting for transfers between devices, gather_window(): lax.ppermute(fwd, 'ctx', [(c, c // z_ring * z_ring + (c % z_ring + 1) % z...  6.25 us
    ppermute x3, starting transfers between devices, gather_window(): stack.append(lax.ppermute(kv, 'ctx', perm))  6.06 us
  transfers between devices with their start and end apart: 20, of which 13 were waited for; matrix products, arithmetic and copies ran while one was open for 6% of the time, Pallas kernels for 0%

profile of v4, /device:TPU:20, one launch (start us, length us, event | category | flops | bytes accessed | tf_op | source)
XLA Modules:
  0.0 188.7 jit_solution(3803060233567921833)
XLA Ops:
  6.5 0.0 copy-start
  6.5 1.6 broadcast_in_dim.31
  8.1 22.8 %all-to-all-start = ((bf16[64,80,24]{1,2,0:T(8,128)(2,1)}), bf16[64,80,24]{1,2,0:T(8,128)(2,1)S(1)}, u32[]{:S(2)}, u32[]{:S(2)}) async-start(bf16[64,80,24]{1,2,0:T(8,128)(2,1)} %broadcast_in_dim.31), calls=%async_computation | async-start | bytes 786432 | tf_op jit(solution)/shard_map/all_to_all | solution.py:154
  30.9 0.0 all-gather.2.cloned.1.call-start
  31.0 0.7 bitcast_convert_fusion.1
  31.7 0.9 multiply_convert_fusion
  32.6 24.6 %all-to-all-done = bf16[64,80,24]{1,2,0:T(8,128)(2,1)S(1)} async-done(((bf16[64,80,24]{1,2,0:T(8,128)(2,1)}), bf16[64,80,24]{1,2,0:T(8,128)(2,1)S(1)}, u32[]{:S(2)}, u32[]{:S(2)}) %all-to-all-start) | async-done | bytes 245792 | tf_op jit(solution)/shard_map/all_to_all | solution.py:154
  57.2 0.1 copy.24
  57.3 1.3 reshape.126
  58.6 0.0 all-gather.2.cloned.1.call-update
  58.6 0.7 collective-permute-start.2
  59.3 4.1 %collective-permute-start = (bf16[128,256]{1,0:T(8,128)(2,1)S(1)}, bf16[128,256]{1,0:T(8,128)(2,1)S(1)}, u32[]{:S(2)}, u32[]{:S(2)}) collective-permute-start(bf16[128,256]{1,0:T(8,128)(2,1)S(1)} %get-tuple-element.10), channel_id=1, source_target_pairs={{0,16},{1,17},{2,18},{3,19},{4,20},{5,21},{6,22},{7,23},{8,24},{9,... | collective-permute-start | bytes 196616 | tf_op jit(solution)/shard_map/ppermute | solution.py:122
  63.4 1.3 collective-permute-start.1
  64.8 0.7 and_select_fusion
  65.5 0.1 add_multiply_fusion
  65.5 1.3 fusion.1
  66.8 0.6 broadcast_bitcast_fusion
  67.5 0.0 collective-permute-done.2
  67.5 0.0 collective-permute-done
  67.5 3.0 %collective-permute-done.1 = bf16[128,256]{1,0:T(8,128)(2,1)S(1)} collective-permute-done((bf16[128,256]{1,0:T(8,128)(2,1)S(1)}, bf16[128,256]{1,0:T(8,128)(2,1)S(1)}, u32[]{:S(2)}, u32[]{:S(2)}) %collective-permute-start.1) | collective-permute-done | bytes 65568 | tf_op jit(solution)/shard_map/ppermute | solution.py:122
  70.5 2.8 %collective-permute-start.3 = (bf16[4,128,256]{2,1,0:T(8,128)(2,1)S(1)}, bf16[4,128,256]{2,1,0:T(8,128)(2,1)S(1)}, u32[]{:S(2)}, u32[]{:S(2)}) collective-permute-start(bf16[4,128,256]{2,1,0:T(8,128)(2,1)S(1)} %pad_maximum_fusion), channel_id=1, source_target_pairs={{0,1},{1,2},{2,3},{3,4},{4,5},{5,6},{6,7},{7,8},{8,9},{9,10},{10,1... | collective-permute-start | bytes 786440 | tf_op jit(solution)/shard_map/ppermute | solution.py:129
  73.3 1.3 broadcast_bitcast_fusion.1
  74.6 0.8 copy.34
  75.4 0.8 copy.32
  76.3 1.8 pad_add_fusion.bound_ref
  78.1 4.3 %collective-permute-start.4 = (bf16[4,128,256]{2,1,0:T(8,128)(2,1)S(1)}, bf16[4,128,256]{2,1,0:T(8,128)(2,1)S(1)}, u32[]{:S(2)}, u32[]{:S(2)}) collective-permute-start(bf16[4,128,256]{2,1,0:T(8,128)(2,1)S(1)} %pad_maximum_fusion), channel_id=1, source_target_pairs={{0,15},{1,0},{2,1},{3,2},{4,3},{5,4},{6,5},{7,6},{8,7},{9,8},{10,9... | collective-permute-start | bytes 786440 | tf_op jit(solution)/shard_map/ppermute | solution.py:135
  82.4 0.0 collective-permute-done.3
  82.4 1.9 %collective-permute-start.5 = (bf16[4,128,256]{2,1,0:T(8,128)(2,1)S(1)}, bf16[4,128,256]{2,1,0:T(8,128)(2,1)S(1)}, u32[]{:S(2)}, u32[]{:S(2)}) collective-permute-start(bf16[4,128,256]{2,1,0:T(8,128)(2,1)S(1)} %collective-permute-done.3), channel_id=1, source_target_pairs={{0,1},{1,2},{2,3},{3,4},{4,5},{5,6},{6,7},{7,8},{8,9},{9,10},{10,1... | collective-permute-start | bytes 786440 | tf_op jit(solution)/shard_map/ppermute | solution.py:129
  84.3 2.0 %collective-permute-done.4 = bf16[4,128,256]{2,1,0:T(8,128)(2,1)S(1)} collective-permute-done((bf16[4,128,256]{2,1,0:T(8,128)(2,1)S(1)}, bf16[4,128,256]{2,1,0:T(8,128)(2,1)S(1)}, u32[]{:S(2)}, u32[]{:S(2)}) %collective-permute-start.4) | collective-permute-done | bytes 262176 | tf_op jit(solution)/shard_map/ppermute | solution.py:135
  86.3 5.5 %collective-permute-start.6 = (bf16[4,128,256]{2,1,0:T(8,128)(2,1)S(1)}, bf16[4,128,256]{2,1,0:T(8,128)(2,1)S(1)}, u32[]{:S(2)}, u32[]{:S(2)}) collective-permute-start(bf16[4,128,256]{2,1,0:T(8,128)(2,1)S(1)} %collective-permute-done.4), channel_id=1, source_target_pairs={{0,15},{1,0},{2,1},{3,2},{4,3},{5,4},{6,5},{7,6},{8,7},{9,8},{10,9... | collective-permute-start | bytes 786440 | tf_op jit(solution)/shard_map/ppermute | solution.py:135
  91.8 0.0 collective-permute-done.5
  91.8 1.9 %collective-permute-start.7 = (bf16[4,128,256]{2,1,0:T(8,128)(2,1)S(1)}, bf16[4,128,256]{2,1,0:T(8,128)(2,1)S(1)}, u32[]{:S(2)}, u32[]{:S(2)}) collective-permute-start(bf16[4,128,256]{2,1,0:T(8,128)(2,1)S(1)} %collective-permute-done.5), channel_id=1, source_target_pairs={{0,1},{1,2},{2,3},{3,4},{4,5},{5,6},{6,7},{7,8},{8,9},{9,10},{10,1... | collective-permute-start | bytes 786440 | tf_op jit(solution)/shard_map/ppermute | solution.py:129
  93.8 1.9 collective-permute-done.6
  95.7 5.6 %collective-permute-start.8 = (bf16[4,128,256]{2,1,0:T(8,128)(2,1)S(1)}, bf16[4,128,256]{2,1,0:T(8,128)(2,1)S(1)}, u32[]{:S(2)}, u32[]{:S(2)}) collective-permute-start(bf16[4,128,256]{2,1,0:T(8,128)(2,1)S(1)} %collective-permute-done.6), channel_id=1, source_target_pairs={{0,15},{1,0},{2,1},{3,2},{4,3},{5,4},{6,5},{7,6},{8,7},{9,8},{10,9... | collective-permute-start | bytes 786440 | tf_op jit(solution)/shard_map/ppermute | solution.py:135
  101.3 0.0 collective-permute-done.7
  101.3 1.9 %collective-permute-start.9 = (bf16[4,128,256]{2,1,0:T(8,128)(2,1)S(1)}, bf16[4,128,256]{2,1,0:T(8,128)(2,1)S(1)}, u32[]{:S(2)}, u32[]{:S(2)}) collective-permute-start(bf16[4,128,256]{2,1,0:T(8,128)(2,1)S(1)} %collective-permute-done.7), channel_id=1, source_target_pairs={{0,1},{1,2},{2,3},{3,4},{4,5},{5,6},{6,7},{7,8},{8,9},{9,10},{10,1... | collective-permute-start | bytes 786440 | tf_op jit(solution)/shard_map/ppermute | solution.py:129
  103.3 2.7 %collective-permute-done.8 = bf16[4,128,256]{2,1,0:T(8,128)(2,1)S(1)} collective-permute-done((bf16[4,128,256]{2,1,0:T(8,128)(2,1)S(1)}, bf16[4,128,256]{2,1,0:T(8,128)(2,1)S(1)}, u32[]{:S(2)}, u32[]{:S(2)}) %collective-permute-start.8) | collective-permute-done | bytes 262176 | tf_op jit(solution)/shard_map/ppermute | solution.py:135
  105.9 5.6 %collective-permute-start.10 = (bf16[4,128,256]{2,1,0:T(8,128)(2,1)S(1)}, bf16[4,128,256]{2,1,0:T(8,128)(2,1)S(1)}, u32[]{:S(2)}, u32[]{:S(2)}) collective-permute-start(bf16[4,128,256]{2,1,0:T(8,128)(2,1)S(1)} %collective-permute-done.8), channel_id=1, source_target_pairs={{0,15},{1,0},{2,1},{3,2},{4,3},{5,4},{6,5},{7,6},{8,7},{9,8},{10,9... | collective-permute-start | bytes 786440 | tf_op jit(solution)/shard_map/ppermute | solution.py:135
  111.6 0.3 collective-permute-done.9
  111.9 1.9 %collective-permute-start.11 = (bf16[4,128,256]{2,1,0:T(8,128)(2,1)S(1)}, bf16[4,128,256]{2,1,0:T(8,128)(2,1)S(1)}, u32[]{:S(2)}, u32[]{:S(2)}) collective-permute-start(bf16[4,128,256]{2,1,0:T(8,128)(2,1)S(1)} %collective-permute-done.9), channel_id=1, source_target_pairs={{0,1},{1,2},{2,3},{3,4},{4,5},{5,6},{6,7},{7,8},{8,9},{9,10},{10,1... | collective-permute-start | bytes 786440 | tf_op jit(solution)/shard_map/ppermute | solution.py:129
  113.8 3.5 %collective-permute-done.10 = bf16[4,128,256]{2,1,0:T(8,128)(2,1)S(1)} collective-permute-done((bf16[4,128,256]{2,1,0:T(8,128)(2,1)S(1)}, bf16[4,128,256]{2,1,0:T(8,128)(2,1)S(1)}, u32[]{:S(2)}, u32[]{:S(2)}) %collective-permute-start.10) | collective-permute-done | bytes 262176 | tf_op jit(solution)/shard_map/ppermute | solution.py:135
  117.3 5.6 %collective-permute-start.12 = (bf16[4,128,256]{2,1,0:T(8,128)(2,1)S(1)}, bf16[4,128,256]{2,1,0:T(8,128)(2,1)S(1)}, u32[]{:S(2)}, u32[]{:S(2)}) collective-permute-start(bf16[4,128,256]{2,1,0:T(8,128)(2,1)S(1)} %collective-permute-done.10), channel_id=1, source_target_pairs={{0,15},{1,0},{2,1},{3,2},{4,3},{5,4},{6,5},{7,6},{8,7},{9,8},{10,9... | collective-permute-start | bytes 786440 | tf_op jit(solution)/shard_map/ppermute | solution.py:135
  123.0 0.2 collective-permute-done.11
  123.2 1.9 %collective-permute-start.13 = (bf16[4,128,256]{2,1,0:T(8,128)(2,1)S(1)}, bf16[4,128,256]{2,1,0:T(8,128)(2,1)S(1)}, u32[]{:S(2)}, u32[]{:S(2)}) collective-permute-start(bf16[4,128,256]{2,1,0:T(8,128)(2,1)S(1)} %collective-permute-done.11), channel_id=1, source_target_pairs={{0,1},{1,2},{2,3},{3,4},{4,5},{5,6},{6,7},{7,8},{8,9},{9,10},{10,1... | collective-permute-start | bytes 786440 | tf_op jit(solution)/shard_map/ppermute | solution.py:129
  125.1 4.4 %collective-permute-done.12 = bf16[4,128,256]{2,1,0:T(8,128)(2,1)S(1)} collective-permute-done((bf16[4,128,256]{2,1,0:T(8,128)(2,1)S(1)}, bf16[4,128,256]{2,1,0:T(8,128)(2,1)S(1)}, u32[]{:S(2)}, u32[]{:S(2)}) %collective-permute-start.12) | collective-permute-done | bytes 262176 | tf_op jit(solution)/shard_map/ppermute | solution.py:135
  129.5 5.6 %collective-permute-start.14 = (bf16[4,128,256]{2,1,0:T(8,128)(2,1)S(1)}, bf16[4,128,256]{2,1,0:T(8,128)(2,1)S(1)}, u32[]{:S(2)}, u32[]{:S(2)}) collective-permute-start(bf16[4,128,256]{2,1,0:T(8,128)(2,1)S(1)} %collective-permute-done.12), channel_id=1, source_target_pairs={{0,15},{1,0},{2,1},{3,2},{4,3},{5,4},{6,5},{7,6},{8,7},{9,8},{10,9... | collective-permute-start | bytes 786440 | tf_op jit(solution)/shard_map/ppermute | solution.py:135
  135.1 0.1 collective-permute-done.13
  135.2 1.9 %collective-permute-start.15 = (bf16[4,128,256]{2,1,0:T(8,128)(2,1)S(1)}, bf16[4,128,256]{2,1,0:T(8,128)(2,1)S(1)}, u32[]{:S(2)}, u32[]{:S(2)}) collective-permute-start(bf16[4,128,256]{2,1,0:T(8,128)(2,1)S(1)} %collective-permute-done.13), channel_id=1, source_target_pairs={{0,1},{1,2},{2,3},{3,4},{4,5},{5,6},{6,7},{7,8},{8,9},{9,10},{10,1... | collective-permute-start | bytes 786440 | tf_op jit(solution)/shard_map/ppermute | solution.py:129
  137.1 4.0 %collective-permute-done.14 = bf16[4,128,256]{2,1,0:T(8,128)(2,1)S(1)} collective-permute-done((bf16[4,128,256]{2,1,0:T(8,128)(2,1)S(1)}, bf16[4,128,256]{2,1,0:T(8,128)(2,1)S(1)}, u32[]{:S(2)}, u32[]{:S(2)}) %collective-permute-start.14) | collective-permute-done | bytes 262176 | tf_op jit(solution)/shard_map/ppermute | solution.py:135
  141.1 5.6 %collective-permute-start.16 = (bf16[4,128,256]{2,1,0:T(8,128)(2,1)S(1)}, bf16[4,128,256]{2,1,0:T(8,128)(2,1)S(1)}, u32[]{:S(2)}, u32[]{:S(2)}) collective-permute-start(bf16[4,128,256]{2,1,0:T(8,128)(2,1)S(1)} %collective-permute-done.14), channel_id=1, source_target_pairs={{0,15},{1,0},{2,1},{3,2},{4,3},{5,4},{6,5},{7,6},{8,7},{9,8},{10,9... | collective-permute-start | bytes 786440 | tf_op jit(solution)/shard_map/ppermute | solution.py:135
  146.8 0.0 collective-permute-done.15
  146.8 1.9 %collective-permute-start.17 = (bf16[4,128,256]{2,1,0:T(8,128)(2,1)S(1)}, bf16[4,128,256]{2,1,0:T(8,128)(2,1)S(1)}, u32[]{:S(2)}, u32[]{:S(2)}) collective-permute-start(bf16[4,128,256]{2,1,0:T(8,128)(2,1)S(1)} %collective-permute-done.15), channel_id=1, source_target_pairs={{0,1},{1,2},{2,3},{3,4},{4,5},{5,6},{6,7},{7,8},{8,9},{9,10},{10,1... | collective-permute-start | bytes 786440 | tf_op jit(solution)/shard_map/ppermute | solution.py:129
  148.7 1.9 collective-permute-done.16
  150.6 5.6 %collective-permute-done.17 = bf16[4,128,256]{2,1,0:T(8,128)(2,1)S(1)} collective-permute-done((bf16[4,128,256]{2,1,0:T(8,128)(2,1)S(1)}, bf16[4,128,256]{2,1,0:T(8,128)(2,1)S(1)}, u32[]{:S(2)}, u32[]{:S(2)}) %collective-permute-start.17) | collective-permute-done | bytes 262176 | tf_op jit(solution)/shard_map/ppermute | solution.py:129
  156.3 2.2 %fusion.7 = (bf16[8192,128]{1,0:T(8,128)(2,1)}, bf16[8192,128]{1,0:T(8,128)(2,1)}) fusion(bf16[8192,256]{1,0:T(8,128)(2,1)S(1)} %bitcast.73), kind=kLoop, calls=%fused_computation.45 | loop fusion | bytes 8388608 | tf_op jit(solution)/shard_map/slice | solution.py:175
  158.5 0.0 all-gather.2.cloned.1.call-done
  158.5 0.0 copy-done
  158.5 3.4 %fusion = bf16[128,384]{1,0:T(8,128)(2,1)S(1)} fusion(bf16[128,5120]{1,0:T(8,128)(2,1)S(1)} %copy-done, bf16[5120,384]{0,1:T(8,128)(2,1)} %all-gather.2.cloned.1.call-done), kind=kOutput, calls=%fused_computation.1 | convolution fusion | flops 503414784 | bytes 5341184 | tf_op jit(solution)/shard_map/dot_general | solution.py:167
  161.9 0.1 copy.25
  162.0 0.8 copy.26
  162.8 17.3 %shard_map.73 = bf16[384,128]{1,0:T(8,128)(2,1)} custom-call(s32[16]{0:T(128)} %get-tuple-element.6.kmin_ref, s32[16]{0:T(128)} %get-tuple-element.5.kmax_ref, s32[2]{0:T(128)} %pad_add_fusion.bound_ref, bf16[384,128]{1,0:T(8,128)(2,1)} %bitcast.78, bf16[8192,128]{1,0:T(8,128)(2,1)} %get-tuple-element.8.k_ref, bf16[8192,128]{1,0:T(8,128)(2,1)} %get-tuple-element.7.v_ref, ...), custom_call_target="tpu_custom_call" | custom-call | tf_op jit(solution)/shard_map/pallas_call | solution.py:63
  180.1 1.0 copy.29
  181.1 0.8 copy.30
  (23 shorter events, 0.4 us)
Async XLA Ops:
  6.5 152.0 %copy-start = (bf16[128,5120]{1,0:T(8,128)(2,1)S(1)}, bf16[128,5120]{1,0:T(8,128)(2,1)}, u32[]{:S(2)}) copy-start(bf16[128,5120]{1,0:T(8,128)(2,1)} %param.7) | copy-start | bytes 3932164
  8.1 49.1 %all-to-all-start = ((bf16[64,80,24]{1,2,0:T(8,128)(2,1)}), bf16[64,80,24]{1,2,0:T(8,128)(2,1)S(1)}, u32[]{:S(2)}, u32[]{:S(2)}) async-start(bf16[64,80,24]{1,2,0:T(8,128)(2,1)} %broadcast_in_dim.31), calls=%async_computation | async-start | bytes 786432 | tf_op jit(solution)/shard_map/all_to_all | solution.py:154
  30.9 127.6 %all-gather.2.cloned.1.call-start = ((), (), s32[]{:S(2)}) async-start(), calls=%async_computation.1 | async-start | bytes 4177920 | tf_op jit(solution)/shard_map/all_gather | solution.py:156
  58.6 8.8 %collective-permute-start.2 = (bf16[128,256]{1,0:T(8,128)(2,1)S(1)}, bf16[128,256]{1,0:T(8,128)(2,1)S(1)}, u32[]{:S(2)}, u32[]{:S(2)}) collective-permute-start(bf16[128,256]{1,0:T(8,128)(2,1)S(1)} %get-tuple-element.10), channel_id=1, source_target_pairs={{0,48},{1,49},{2,50},{3,51},{4,52},{5,53},{6,54},{7,55},{8,56},{9,... | collective-permute-start | bytes 196616 | tf_op jit(solution)/shard_map/ppermute | solution.py:122
  59.3 8.2 %collective-permute-start = (bf16[128,256]{1,0:T(8,128)(2,1)S(1)}, bf16[128,256]{1,0:T(8,128)(2,1)S(1)}, u32[]{:S(2)}, u32[]{:S(2)}) collective-permute-start(bf16[128,256]{1,0:T(8,128)(2,1)S(1)} %get-tuple-element.10), channel_id=1, source_target_pairs={{0,16},{1,17},{2,18},{3,19},{4,20},{5,21},{6,22},{7,23},{8,24},{9,... | collective-permute-start | bytes 196616 | tf_op jit(solution)/shard_map/ppermute | solution.py:122
  63.4 7.1 %collective-permute-start.1 = (bf16[128,256]{1,0:T(8,128)(2,1)S(1)}, bf16[128,256]{1,0:T(8,128)(2,1)S(1)}, u32[]{:S(2)}, u32[]{:S(2)}) collective-permute-start(bf16[128,256]{1,0:T(8,128)(2,1)S(1)} %get-tuple-element.10), channel_id=1, source_target_pairs={{0,32},{1,33},{2,34},{3,35},{4,36},{5,37},{6,38},{7,39},{8,40},{9,... | collective-permute-start | bytes 196616 | tf_op jit(solution)/shard_map/ppermute | solution.py:122
  70.5 11.8 %collective-permute-start.3 = (bf16[4,128,256]{2,1,0:T(8,128)(2,1)S(1)}, bf16[4,128,256]{2,1,0:T(8,128)(2,1)S(1)}, u32[]{:S(2)}, u32[]{:S(2)}) collective-permute-start(bf16[4,128,256]{2,1,0:T(8,128)(2,1)S(1)} %pad_maximum_fusion), channel_id=1, source_target_pairs={{0,1},{1,2},{2,3},{3,4},{4,5},{5,6},{6,7},{7,8},{8,9},{9,10},{10,1... | collective-permute-start | bytes 786440 | tf_op jit(solution)/shard_map/ppermute | solution.py:129
  78.1 8.3 %collective-permute-start.4 = (bf16[4,128,256]{2,1,0:T(8,128)(2,1)S(1)}, bf16[4,128,256]{2,1,0:T(8,128)(2,1)S(1)}, u32[]{:S(2)}, u32[]{:S(2)}) collective-permute-start(bf16[4,128,256]{2,1,0:T(8,128)(2,1)S(1)} %pad_maximum_fusion), channel_id=1, source_target_pairs={{0,15},{1,0},{2,1},{3,2},{4,3},{5,4},{6,5},{7,6},{8,7},{9,8},{10,9... | collective-permute-start | bytes 786440 | tf_op jit(solution)/shard_map/ppermute | solution.py:135
  82.4 9.5 %collective-permute-start.5 = (bf16[4,128,256]{2,1,0:T(8,128)(2,1)S(1)}, bf16[4,128,256]{2,1,0:T(8,128)(2,1)S(1)}, u32[]{:S(2)}, u32[]{:S(2)}) collective-permute-start(bf16[4,128,256]{2,1,0:T(8,128)(2,1)S(1)} %collective-permute-done.3), channel_id=1, source_target_pairs={{0,1},{1,2},{2,3},{3,4},{4,5},{5,6},{6,7},{7,8},{8,9},{9,10},{10,1... | collective-permute-start | bytes 786440 | tf_op jit(solution)/shard_map/ppermute | solution.py:129
  86.3 9.3 %collective-permute-start.6 = (bf16[4,128,256]{2,1,0:T(8,128)(2,1)S(1)}, bf16[4,128,256]{2,1,0:T(8,128)(2,1)S(1)}, u32[]{:S(2)}, u32[]{:S(2)}) collective-permute-start(bf16[4,128,256]{2,1,0:T(8,128)(2,1)S(1)} %collective-permute-done.4), channel_id=1, source_target_pairs={{0,15},{1,0},{2,1},{3,2},{4,3},{5,4},{6,5},{7,6},{8,7},{9,8},{10,9... | collective-permute-start | bytes 786440 | tf_op jit(solution)/shard_map/ppermute | solution.py:135
  91.8 9.5 %collective-permute-start.7 = (bf16[4,128,256]{2,1,0:T(8,128)(2,1)S(1)}, bf16[4,128,256]{2,1,0:T(8,128)(2,1)S(1)}, u32[]{:S(2)}, u32[]{:S(2)}) collective-permute-start(bf16[4,128,256]{2,1,0:T(8,128)(2,1)S(1)} %collective-permute-done.5), channel_id=1, source_target_pairs={{0,1},{1,2},{2,3},{3,4},{4,5},{5,6},{6,7},{7,8},{8,9},{9,10},{10,1... | collective-permute-start | bytes 786440 | tf_op jit(solution)/shard_map/ppermute | solution.py:129
  95.7 10.3 %collective-permute-start.8 = (bf16[4,128,256]{2,1,0:T(8,128)(2,1)S(1)}, bf16[4,128,256]{2,1,0:T(8,128)(2,1)S(1)}, u32[]{:S(2)}, u32[]{:S(2)}) collective-permute-start(bf16[4,128,256]{2,1,0:T(8,128)(2,1)S(1)} %collective-permute-done.6), channel_id=1, source_target_pairs={{0,15},{1,0},{2,1},{3,2},{4,3},{5,4},{6,5},{7,6},{8,7},{9,8},{10,9... | collective-permute-start | bytes 786440 | tf_op jit(solution)/shard_map/ppermute | solution.py:135
  101.3 10.5 %collective-permute-start.9 = (bf16[4,128,256]{2,1,0:T(8,128)(2,1)S(1)}, bf16[4,128,256]{2,1,0:T(8,128)(2,1)S(1)}, u32[]{:S(2)}, u32[]{:S(2)}) collective-permute-start(bf16[4,128,256]{2,1,0:T(8,128)(2,1)S(1)} %collective-permute-done.7), channel_id=1, source_target_pairs={{0,1},{1,2},{2,3},{3,4},{4,5},{5,6},{6,7},{7,8},{8,9},{9,10},{10,1... | collective-permute-start | bytes 786440 | tf_op jit(solution)/shard_map/ppermute | solution.py:129
  105.9 11.4 %collective-permute-start.10 = (bf16[4,128,256]{2,1,0:T(8,128)(2,1)S(1)}, bf16[4,128,256]{2,1,0:T(8,128)(2,1)S(1)}, u32[]{:S(2)}, u32[]{:S(2)}) collective-permute-start(bf16[4,128,256]{2,1,0:T(8,128)(2,1)S(1)} %collective-permute-done.8), channel_id=1, source_target_pairs={{0,15},{1,0},{2,1},{3,2},{4,3},{5,4},{6,5},{7,6},{8,7},{9,8},{10,9... | collective-permute-start | bytes 786440 | tf_op jit(solution)/shard_map/ppermute | solution.py:135
  111.9 11.3 %collective-permute-start.11 = (bf16[4,128,256]{2,1,0:T(8,128)(2,1)S(1)}, bf16[4,128,256]{2,1,0:T(8,128)(2,1)S(1)}, u32[]{:S(2)}, u32[]{:S(2)}) collective-permute-start(bf16[4,128,256]{2,1,0:T(8,128)(2,1)S(1)} %collective-permute-done.9), channel_id=1, source_target_pairs={{0,1},{1,2},{2,3},{3,4},{4,5},{5,6},{6,7},{7,8},{8,9},{9,10},{10,1... | collective-permute-start | bytes 786440 | tf_op jit(solution)/shard_map/ppermute | solution.py:129
  117.3 12.2 %collective-permute-start.12 = (bf16[4,128,256]{2,1,0:T(8,128)(2,1)S(1)}, bf16[4,128,256]{2,1,0:T(8,128)(2,1)S(1)}, u32[]{:S(2)}, u32[]{:S(2)}) collective-permute-start(bf16[4,128,256]{2,1,0:T(8,128)(2,1)S(1)} %collective-permute-done.10), channel_id=1, source_target_pairs={{0,15},{1,0},{2,1},{3,2},{4,3},{5,4},{6,5},{7,6},{8,7},{9,8},{10,9... | collective-permute-start | bytes 786440 | tf_op jit(solution)/shard_map/ppermute | solution.py:135
  123.2 12.0 %collective-permute-start.13 = (bf16[4,128,256]{2,1,0:T(8,128)(2,1)S(1)}, bf16[4,128,256]{2,1,0:T(8,128)(2,1)S(1)}, u32[]{:S(2)}, u32[]{:S(2)}) collective-permute-start(bf16[4,128,256]{2,1,0:T(8,128)(2,1)S(1)} %collective-permute-done.11), channel_id=1, source_target_pairs={{0,1},{1,2},{2,3},{3,4},{4,5},{5,6},{6,7},{7,8},{8,9},{9,10},{10,1... | collective-permute-start | bytes 786440 | tf_op jit(solution)/shard_map/ppermute | solution.py:129
  129.5 11.6 %collective-permute-start.14 = (bf16[4,128,256]{2,1,0:T(8,128)(2,1)S(1)}, bf16[4,128,256]{2,1,0:T(8,128)(2,1)S(1)}, u32[]{:S(2)}, u32[]{:S(2)}) collective-permute-start(bf16[4,128,256]{2,1,0:T(8,128)(2,1)S(1)} %collective-permute-done.12), channel_id=1, source_target_pairs={{0,15},{1,0},{2,1},{3,2},{4,3},{5,4},{6,5},{7,6},{8,7},{9,8},{10,9... | collective-permute-start | bytes 786440 | tf_op jit(solution)/shard_map/ppermute | solution.py:135
  135.2 11.6 %collective-permute-start.15 = (bf16[4,128,256]{2,1,0:T(8,128)(2,1)S(1)}, bf16[4,128,256]{2,1,0:T(8,128)(2,1)S(1)}, u32[]{:S(2)}, u32[]{:S(2)}) collective-permute-start(bf16[4,128,256]{2,1,0:T(8,128)(2,1)S(1)} %collective-permute-done.13), channel_id=1, source_target_pairs={{0,1},{1,2},{2,3},{3,4},{4,5},{5,6},{6,7},{7,8},{8,9},{9,10},{10,1... | collective-permute-start | bytes 786440 | tf_op jit(solution)/shard_map/ppermute | solution.py:129
  141.1 9.5 %collective-permute-start.16 = (bf16[4,128,256]{2,1,0:T(8,128)(2,1)S(1)}, bf16[4,128,256]{2,1,0:T(8,128)(2,1)S(1)}, u32[]{:S(2)}, u32[]{:S(2)}) collective-permute-start(bf16[4,128,256]{2,1,0:T(8,128)(2,1)S(1)} %collective-permute-done.14), channel_id=1, source_target_pairs={{0,15},{1,0},{2,1},{3,2},{4,3},{5,4},{6,5},{7,6},{8,7},{9,8},{10,9... | collective-permute-start | bytes 786440 | tf_op jit(solution)/shard_map/ppermute | solution.py:135
  146.8 9.5 %collective-permute-start.17 = (bf16[4,128,256]{2,1,0:T(8,128)(2,1)S(1)}, bf16[4,128,256]{2,1,0:T(8,128)(2,1)S(1)}, u32[]{:S(2)}, u32[]{:S(2)}) collective-permute-start(bf16[4,128,256]{2,1,0:T(8,128)(2,1)S(1)} %collective-permute-done.15), channel_id=1, source_target_pairs={{0,1},{1,2},{2,3},{3,4},{4,5},{5,6},{6,7},{7,8},{8,9},{9,10},{10,1... | collective-permute-start | bytes 786440 | tf_op jit(solution)/shard_map/ppermute | solution.py:129
Sparse Core Ops, SparseCore 0:
  58.7 80.1 all-gather.1
